TPU v7x, 256 devices: a whole 4x4x8 slice. The times are simulated.
256 devices in a mesh: seq: 32 (over y, x, core), dp: 8 (over z).
Axes of the slice: x: 4, y: 4, z: 8, core: 2. Of those that a mesh axis runs over, the one named last changes fastest.
Arguments:
- query_rows: bfloat16 [8, 8192, 2048], P('dp', 'seq'), may hold values from -200 to 200
- key_rows: bfloat16 [8, 8192, 256], P('dp', 'seq'), may hold values from -6 to 6
- value_rows: bfloat16 [8, 8192, 256], P('dp', 'seq'), may hold values from -8 to 8
- file_lengths: int32 [8, 32], P('dp'), may hold values from 1 to 512, 8192 in all within a row
- residual: bfloat16 [8, 8192, 2048], P('dp', 'seq'), may hold values from -36 to 36
- w_out: bfloat16 [2048, 2048], P(None, 'dp'), may hold values from -0.125 to 0.125
- norm_gain: float32 [2048], replicated, may hold values from 0.25 to 1.75
- routes: int32 [8, 8192, 2], P('dp', 'seq'), may hold values from 0 to 31, all different within a row; in each aligned block of 256 rows (0 to 255, 256 to 511, ..., all dimensions but the last counted through in order) at most 24 rows name the same one
- route_gates: float32 [8, 8192, 2], P('dp', 'seq'), may hold values from 0.1 to 0.6
- w_gate: bfloat16 [32, 2048, 384], P('seq'), may hold values from -0.125 to 0.125
- w_up: bfloat16 [32, 2048, 384], P('seq'), may hold values from -0.125 to 0.125
- w_down: bfloat16 [32, 384, 2048], P('seq'), may hold values from -0.3125 to 0.3125
- cotangent: bfloat16 [8, 8192, 2048], P('dp', 'seq'), may hold values from -6 to 6
Outputs:
- layer_out: bfloat16 [8, 8192, 2048], P('dp', 'seq')
- grad_stream: bfloat16 [8, 8192, 2048], P('dp', 'seq')
- grad_gate: bfloat16 [32, 2048, 384], P('seq', 'dp')
- grad_up: bfloat16 [32, 2048, 384], P('seq', 'dp')
- grad_down: bfloat16 [32, 384, 2048], P('seq', None, 'dp')
Inputs may be any that keep to these rules, and one draw needn't show every extreme that they name: `file_lengths`: each batch's 32 file lengths sum to 8192; the longest is exactly 512. `routes`: each token names 2 different experts. Among the tokens of one device no expert is named more than 24 times, and in every draw some device names some expert exactly 24 times.
All inputs are finite; a program needn't handle non-finite values.
Results may differ from a plain program's by a relative error of at most 0.022.
Values may be sent and summed in bfloat16 or wider, within the bound.
No kernel may reach another device: no remote copies, remote signals or barrier semaphores. Data moves between devices by JAX's collectives and lax.ppermute only.
A program may use at most 128 MiB of HBM per device.

v0:
```python
import jax
import jax.numpy as jnp
from jax import lax
from jax.sharding import PartitionSpec as P

HEADS = 16
KV = 2
HD = 128
TOP = 2
HOPS = 2
FILE_MAX = 512


epsilon = 1e-06
masked = -1e30


def from_behind(shard, axis, by):
    peers = lax.axis_size(axis)
    pairs = [(i, i + by) for i in range(peers) if 0 <= i + by < peers]
    return lax.ppermute(shard, axis, pairs)


def normed(stream, gain):
    inverse = lax.rsqrt(jnp.mean(stream * stream, axis=-1, keepdims=True) + epsilon)
    return stream * inverse * gain


def file_index(places, ends):
    hits = (ends[None, :] <= places[:, None]).astype(jnp.int32)
    return jnp.sum(hits, axis=1)


def slot_targets(chosen, experts_all, capacity):
    flat_ids = chosen.reshape(-1)
    onehot = (flat_ids[:, None] == jnp.arange(experts_all, dtype=jnp.int32)[None, :]).astype(
        jnp.int32
    )
    earlier = jnp.cumsum(onehot, axis=0) - onehot
    placed = jnp.sum(earlier * onehot, axis=1)
    return flat_ids * capacity + placed


def attend_block(queries, keys_all, values_all, query_files, key_files, query_places, key_places):
    row_count = queries.shape[0]
    groups = HEADS // KV
    grouped = queries.reshape(row_count, KV, groups, HD)
    scores = jnp.einsum(
        "rkgd,skd->kgrs", grouped, keys_all.reshape(-1, KV, HD), preferred_element_type=jnp.float32
    ) * HD ** (-0.5)
    allowed = (
        (query_files[:, None] == key_files[None, :])
        & (key_places[None, :] <= query_places[:, None])
        & (key_places[None, :] >= 0)
    )
    scores = jnp.where(allowed, scores, masked)
    row_max = jnp.max(scores, axis=-1, keepdims=True)
    raised = jnp.exp(scores - row_max)
    probs = (raised / jnp.sum(raised, axis=-1, keepdims=True)).astype(jnp.bfloat16)
    mixed = jnp.einsum(
        "kgrs,skd->rkgd", probs, values_all.reshape(-1, KV, HD), preferred_element_type=jnp.float32
    )
    return mixed.reshape(row_count, HEADS * HD).astype(jnp.bfloat16)


def expert_forward(inputs, w_gate, w_up, w_down):
    pre_gate = jnp.einsum("secd,edf->secf", inputs, w_gate, preferred_element_type=jnp.float32)
    pre_up = jnp.einsum("secd,edf->secf", inputs, w_up, preferred_element_type=jnp.float32)
    hidden = (jax.nn.silu(pre_gate) * pre_up).astype(jnp.bfloat16)
    result = jnp.einsum(
        "secf,efd->secd", hidden, w_down, preferred_element_type=jnp.float32
    ).astype(jnp.bfloat16)
    return (pre_gate, pre_up, hidden, result)


def expert_backward(inputs, grads_in, pre_gate, pre_up, hidden, w_gate, w_up, w_down):
    grad_down = jnp.einsum("secf,secd->efd", hidden, grads_in, preferred_element_type=jnp.float32)
    grad_hidden = jnp.einsum("secd,efd->secf", grads_in, w_down, preferred_element_type=jnp.float32)
    sigma = jax.nn.sigmoid(pre_gate)
    grad_pre_gate = (grad_hidden * pre_up * sigma * (1.0 + pre_gate * (1.0 - sigma))).astype(
        jnp.bfloat16
    )
    grad_pre_up = (grad_hidden * pre_gate * sigma).astype(jnp.bfloat16)
    grad_gate = jnp.einsum(
        "secd,secf->edf", inputs, grad_pre_gate, preferred_element_type=jnp.float32
    )
    grad_up = jnp.einsum("secd,secf->edf", inputs, grad_pre_up, preferred_element_type=jnp.float32)
    grad_inputs = jnp.einsum(
        "secf,edf->secd", grad_pre_gate, w_gate, preferred_element_type=jnp.float32
    )
    grad_inputs = grad_inputs + jnp.einsum(
        "secf,edf->secd", grad_pre_up, w_up, preferred_element_type=jnp.float32
    )
    return (grad_gate, grad_up, grad_down, grad_inputs.astype(jnp.bfloat16))


def body(
    query_rows,
    key_rows,
    value_rows,
    file_lengths,
    residual,
    w_out,
    norm_gain,
    routes,
    route_gates,
    w_gate,
    w_up,
    w_down,
    cotangent,
):
    tokens = query_rows.shape[1]
    width = residual.shape[2]
    seq_count = lax.axis_size("seq")
    owned = w_gate.shape[0]
    experts_all = owned * seq_count
    capacity = max(2, 3 * tokens * TOP // (2 * experts_all))
    slots = experts_all * capacity
    seq_index = lax.axis_index("seq")
    position = seq_index * tokens

    targets = slot_targets(routes[0], experts_all, capacity)
    route_select = (
        targets[None, :] == jnp.arange(slots, dtype=jnp.int32)[:, None]
    ).astype(jnp.bfloat16)
    token_select = route_select.reshape(slots, tokens, TOP).sum(axis=2)
    sent_shape = (seq_count, owned * capacity, width)
    owner_shape = (seq_count, owned, capacity, width)

    slot_grad = (route_gates[0][:, :, None] * cotangent[0].astype(jnp.float32)[:, None, :]).astype(
        jnp.bfloat16
    )
    grads_outgoing = (
        jnp.dot(route_select, slot_grad.reshape(tokens * TOP, width), preferred_element_type=jnp.float32)
        .astype(jnp.bfloat16)
        .reshape(sent_shape)
    )
    grads_arrived = lax.all_to_all(
        grads_outgoing, "seq", split_axis=0, concat_axis=0, tiled=True
    ).reshape(owner_shape)

    rows_in = w_out.shape[0]
    half = rows_in // 2
    core = seq_index % 2
    mine = lax.all_gather(
        lax.dynamic_slice_in_dim(w_out, core * half, half, axis=0), "dp", axis=1, tiled=True
    )

    own_keys = key_rows[0]
    own_values = value_rows[0]
    own_pair = jnp.stack([own_keys, own_values])
    key_parts = []
    value_parts = []
    for distance in range(HOPS, 0, -1):
        earlier_pair = from_behind(own_pair, "seq", distance)
        key_parts.append(earlier_pair[0])
        value_parts.append(earlier_pair[1])
    keys_all = jnp.concatenate(key_parts + [own_keys], axis=0)
    values_all = jnp.concatenate(value_parts + [own_values], axis=0)
    ends = jnp.cumsum(file_lengths[0])
    query_places = position + jnp.arange(tokens, dtype=jnp.int32)
    key_places = position - FILE_MAX + jnp.arange(tokens + FILE_MAX, dtype=jnp.int32)
    attended = attend_block(
        query_rows[0],
        keys_all,
        values_all,
        file_index(query_places, ends),
        file_index(key_places, ends),
        query_places,
        key_places,
    )
    grads_arrived, mine, attended = lax.optimization_barrier((grads_arrived, mine, attended))
    other = lax.ppermute(mine, "seq", [(i, i ^ 1) for i in range(seq_count)])
    attended_mine = lax.dynamic_slice_in_dim(attended, core * half, half, axis=1)
    attended_other = lax.dynamic_slice_in_dim(attended, (1 - core) * half, half, axis=1)
    projected = (
        jnp.dot(attended_mine, mine, preferred_element_type=jnp.float32)
        + jnp.dot(attended_other, other, preferred_element_type=jnp.float32)
    ).astype(jnp.bfloat16)
    stream = residual[0].astype(jnp.float32) + projected.astype(jnp.float32)
    normalized = normed(stream, norm_gain).astype(jnp.bfloat16)
    outgoing = (
        jnp.dot(token_select, normalized, preferred_element_type=jnp.float32)
        .astype(jnp.bfloat16)
        .reshape(sent_shape)
    )
    arrived = lax.all_to_all(outgoing, "seq", split_axis=0, concat_axis=0, tiled=True).reshape(
        owner_shape
    )
    pre_gate, pre_up, hidden, expert_out = expert_forward(arrived, w_gate, w_up, w_down)
    returned = lax.all_to_all(
        expert_out.reshape(sent_shape), "seq", split_axis=0, concat_axis=0, tiled=True
    )
    grad_gate, grad_up, grad_down, grad_inputs = expert_backward(
        arrived, grads_arrived, pre_gate, pre_up, hidden, w_gate, w_up, w_down
    )
    returned, grad_inputs = lax.optimization_barrier((returned, grad_inputs))
    grads_returned = lax.all_to_all(
        grad_inputs.reshape(sent_shape), "seq", split_axis=0, concat_axis=0, tiled=True
    )
    expert_rows = lax.dot_general(
        route_select,
        returned.reshape(slots, width),
        (((0,), (0,)), ((), ())),
        preferred_element_type=jnp.float32,
    ).reshape(tokens, TOP, width)
    mixture = jnp.sum(route_gates[0][:, :, None] * expert_rows, axis=1)
    layer_out = (stream + mixture).astype(jnp.bfloat16)
    grad_normalized = lax.dot_general(
        token_select,
        grads_returned.reshape(slots, width),
        (((0,), (0,)), ((), ())),
        preferred_element_type=jnp.float32,
    )
    pullback = jax.vjp(lambda inner: normed(inner, norm_gain), stream)[1]
    grad_stream = (cotangent[0].astype(jnp.float32) + pullback(grad_normalized)[0]).astype(
        jnp.bfloat16
    )
    gate_up = lax.psum_scatter(
        jnp.concatenate([grad_gate.astype(jnp.bfloat16), grad_up.astype(jnp.bfloat16)], axis=0),
        "dp",
        scatter_dimension=1,
        tiled=True,
    )
    down = lax.psum_scatter(grad_down.astype(jnp.bfloat16), "dp", scatter_dimension=2, tiled=True)
    return (
        layer_out[None],
        grad_stream[None],
        gate_up[:owned],
        gate_up[owned:],
        down,
    )


def solution(mesh):
    return jax.shard_map(
        body,
        mesh=mesh,
        in_specs=(
            P("dp", "seq", None),
            P("dp", "seq", None),
            P("dp", "seq", None),
            P("dp", None),
            P("dp", "seq", None),
            P(None, "dp"),
            P(),
            P("dp", "seq", None),
            P("dp", "seq", None),
            P("seq", None, None),
            P("seq", None, None),
            P("seq", None, None),
            P("dp", "seq", None),
        ),
        out_specs=(
            P("dp", "seq", None),
            P("dp", "seq", None),
            P("seq", "dp", None),
            P("seq", "dp", None),
            P("seq", None, "dp"),
        ),
        check_vma=False,
    )
```

profile of v0, /device:TPU:32, one launch (start us, length us, event | category | flops | bytes accessed | tf_op | source)
XLA Modules:
  0.0 268.0 jit_solution(12956072962757764070)
XLA Ops:
  7.2 0.0 all-gather.2.cloned.1.call-start
  7.3 2.0 constant_dynamic-slice_fusion
  9.3 0.0 all-gather.2.cloned.1.call-update
  9.3 1.0 copy.77
  10.3 1.0 copy.78
  11.4 4.1 %collective-permute-start = (bf16[2,256,256]{1,2,0:T(8,128)(2,1)S(1)}, bf16[2,256,256]{1,2,0:T(8,128)(2,1)}, u32[]{:S(2)}, u32[]{:S(2)}) collective-permute-start(bf16[2,256,256]{1,2,0:T(8,128)(2,1)S(1)} %pad_maximum_fusion.1), channel_id=1, source_target_pairs={{0,16},{8,24},{16,32},{24,40},{32,48},{40,56},{48,64},{56,72},{64,... | collective-permute-start | bytes 786440 | tf_op jit(solution)/shard_map/ppermute | solution.py:21
  15.5 2.2 collective-permute-start.1
  17.6 0.1 copy.73
  17.8 0.1 eq.80
  17.9 0.1 reshape_squeeze.6
  18.1 1.2 reduce-window.18
  19.3 0.2 slice_reduce_fusion
  19.5 0.2 bitcast_convert_fusion.3
  19.8 4.4 %mul.153 = f32[256,2,2048]{2,1,0:T(2,128)} broadcast(f32[256,2048]{1,0:T(8,128)S(1)} %bitcast_convert_fusion.3), dimensions={0,2} | broadcast | bytes 6291456 | tf_op jit(solution)/shard_map/mul | solution.py:130
  24.2 6.1 %mul.154 = f32[512,2048]{1,0:T(8,128)} reshape(f32[256,2,2048]{2,1,0:T(2,128)} %mul.153) | data formatting | bytes 8388608 | tf_op jit(solution)/shard_map/mul | solution.py:130
  30.3 0.1 copy.76
  30.4 0.1 mul.151
  30.5 0.1 fusion.79
  30.7 5.8 %convolution_convert_fusion.2 = bf16[768,2048]{1,0:T(8,128)(2,1)} fusion(f32[512,2048]{1,0:T(8,128)} %mul.154, f32[512]{0:T(512)S(1)} %mul.151, s32[512]{0:T(512)S(1)} %multiply_add_fusion), kind=kOutput, calls=%fused_computation.14 | convolution fusion | flops 1614675968 | bytes 7344128 | tf_op jit(solution)/shard_map/dot_general | solution.py:134
  36.5 7.3 %all-to-all-start = ((bf16[32,24,2048]{2,1,0:T(8,128)(2,1)}), bf16[32,24,2048]{2,1,0:T(8,128)(2,1)}, u32[]{:S(2)}, u32[]{:S(2)}) async-start(bf16[32,24,2048]{2,1,0:T(8,128)(2,1)} %bitcast.195), calls=%async_computation | async-start | bytes 6291456 | tf_op jit(solution)/shard_map/all_to_all | solution.py:138
  43.8 0.2 reduce-scatter.3.cloned.1.call-start
  44.0 0.1 copy.80
  44.1 0.1 reduce-window.20
  44.2 0.1 reduce.2
  44.3 0.1 convert_reduce_fusion.1
  44.4 0.1 convert_reduce_fusion
  44.5 0.7 and_and_fusion
  45.3 0.8 copy.84
  46.0 2.4 copy.94
  48.5 1.6 fusion.92
  50.1 0.8 copy.82
  50.9 1.0 fusion.93
  51.9 0.1 copy.83
  52.0 10.2 %fusion.94 = (f32[2,8,256]{2,1,0:T(8,128)S(1)}, f32[2,8,256,768]{2,3,1,0:T(8,128)}) fusion(pred[256,768]{0,1:T(8,128)(4,1)S(1)} %and_and_fusion, bf16[256,2,8,128]{3,2,1,0:T(8,128)(2,1)} %bitcast.198, bf16[256,2,128]{2,0,1:T(8,128)(2,1)} %copy.84, bf16[256,2,128]{2,0,1:T(8,128)(2,1)S(1)} %copy.83, bf16[256,2,128]{2,0,1:T(8,128)(2,1)} %copy.82), kind=kOutput, calls=%fused_computation.121 | convolution fusion | flops 819069696 | bytes 14237696 | tf_op jit(solution)/shard_map/sub | solution.py:58
  62.2 6.7 %fusion.36 = bf16[2,128,8,256]{3,1,2,0:T(8,128)(2,1)} fusion(f32[2,8,256,768]{2,3,1,0:T(8,128)} %get-tuple-element.27, f32[2,8,256]{2,1,0:T(8,128)S(1)} %get-tuple-element.26, bf16[256,2,128]{0,2,1:T(8,128)(2,1)S(1)} %bitcast.199, bf16[256,2,128]{0,2,1:T(8,128)(2,1)S(1)} %bitcast.205, bf16[256,2,128]{0,2,1:T(8,128)(2,1)S(1)} %bitcast.204), kind=kOutput, calls=%fused_computation.54 | convolution fusion | flops 813301760 | bytes 14041088 | tf_op jit(solution)/shard_map/kgrs,skd->rkgd/dot_general | solution.py:60
  68.9 16.9 %all-to-all-done = bf16[32,24,2048]{2,1,0:T(8,128)(2,1)} async-done(((bf16[32,24,2048]{2,1,0:T(8,128)(2,1)}), bf16[32,24,2048]{2,1,0:T(8,128)(2,1)}, u32[]{:S(2)}, u32[]{:S(2)}) %all-to-all-start) | async-done | bytes 3145760 | tf_op jit(solution)/shard_map/all_to_all | solution.py:138
  85.8 0.1 reduce_sum.89
  86.0 0.1 copy.88
  86.0 0.3 fusion.61
  86.4 3.8 %fusion.71 = f32[256,2048]{1,0:T(8,128)S(1)} fusion(bf16[1024,2048]{1,0:T(8,128)(2,1)} %all-gather.2.cloned.1.call-done, bf16[256,2048]{0,1:T(8,128)(2,1)} %bitcast.202, s32[]{:T(128)S(6)} %select_n.19), kind=kOutput, calls=%fused_computation.82 | convolution fusion | flops 1073741824 | bytes 6815748 | tf_op jit(solution)/shard_map/dot_general | solution.py:177
  90.2 3.1 %collective-permute-done.2 = bf16[1024,2048]{1,0:T(8,128)(2,1)} collective-permute-done((bf16[1024,2048]{1,0:T(8,128)(2,1)}, bf16[1024,2048]{1,0:T(8,128)(2,1)}, u32[]{:S(2)}, u32[]{:S(2)}) %collective-permute-start.2) | collective-permute-done | bytes 4194336 | tf_op jit(solution)/shard_map/ppermute | solution.py:173
  93.3 3.7 %multiply_reduce_fusion.2 = (f32[256]{0:T(256)S(1)}, f32[256,2048]{1,0:T(8,128)S(1)}) fusion(f32[256,2048]{1,0:T(8,128)S(1)} %fusion.71, bf16[1024,2048]{1,0:T(8,128)(2,1)} %collective-permute-done.2, bf16[256,2048]{0,1:T(8,128)(2,1)S(1)} %bitcast.203, s32[]{:T(128)S(6)} %select_n.21, bf16[1,256,2048]{2,1,0:T(8,128)(2,1)S(1)} %copy-done.8), kind=kOutput, calls=%fused_computation.38 | convolution fusion | flops 1077411584 | bytes 9962500 | tf_op jit(solution)/shard_map/dot_general | solution.py:178
  97.0 1.1 convolution_convert_fusion.1
  98.1 0.2 copy-done.1
  98.4 42.8 %all_to_all.20 = bf16[32,24,2048]{2,1,0:T(8,128)(2,1)S(1)} all-to-all(bf16[32,24,2048]{2,1,0:T(8,128)(2,1)S(1)} %bitcast.193), channel_id=1, replica_groups=mesh['seq'=32,'dp'=8] {'seq'}, dimensions={0} | all-to-all | bytes 6291456 | tf_op jit(solution)/shard_map/all_to_all | solution.py:187
  141.2 1.8 fusion.37
  143.0 1.8 fusion.40
  144.9 4.9 %multiply_convert_fusion.3 = (bf16[32,1,24,384]{3,2,0,1:T(8,128)(2,1)S(1)}, bf16[32,1,24,384]{3,2,0,1:T(8,128)(2,1)S(1)}, bf16[32,1,24,384]{3,2,0,1:T(8,128)(2,1)}) fusion(f32[32,1,24,384]{3,2,0,1:T(8,128)S(1)} %fusion.37, f32[32,1,24,384]{3,2,0,1:T(8,128)S(1)} %fusion.40, bf16[1,384,2048]{2,1,0:T(8,128)(2,1)S(1)} %copy-done, ...), kind=kOutput, calls=%fused_computation.59 | convolution fusion | flops 1212678144 | bytes 8847360 | tf_op jit(solution)/shard_map/secd,efd->secf/dot_general | solution.py:78
  149.8 1.9 fusion.13
  151.7 1.9 fusion.14
  153.6 2.0 pad_maximum_fusion
  155.6 4.5 %convolution_convert_fusion = bf16[32,24,2048]{2,1,0:T(8,128)(2,1)} fusion(bf16[1,384,2048]{2,1,0:T(8,128)(2,1)S(1)} %copy-done, bf16[32,1,24,384]{3,2,0,1:T(8,128)(2,1)} %get-tuple-element.17), kind=kOutput, calls=%fused_computation.12 | convolution fusion | flops 1209532416 | bytes 5308416 | tf_op jit(solution)/shard_map/secf,efd->secd/dot_general | solution.py:70
  160.1 5.1 %all-to-all-start.2 = ((bf16[32,24,2048]{2,1,0:T(8,128)(2,1)}), bf16[32,24,2048]{2,1,0:T(8,128)(2,1)}, u32[]{:S(2)}, u32[]{:S(2)}) async-start(bf16[32,24,2048]{2,1,0:T(8,128)(2,1)} %convolution_convert_fusion), calls=%async_computation.2 | async-start | bytes 6291456 | tf_op jit(solution)/shard_map/all_to_all | solution.py:191
  165.2 3.8 %fusion.29 = f32[32,24,2048]{2,1,0:T(8,128)S(1)} fusion(bf16[1,2048,384]{2,1,0:T(8,128)(2,1)} %param.22, bf16[32,1,24,384]{3,2,0,1:T(8,128)(2,1)} %copy-done.11), kind=kOutput, calls=%fused_computation.45 | convolution fusion | flops 1207959552 | bytes 8454144 | tf_op jit(solution)/shard_map/secf,edf->secd/dot_general | solution.py:88
  169.0 3.6 %fusion.10 = bf16[32,1,24,2048]{3,2,0,1:T(8,128)(2,1)} fusion(f32[32,24,2048]{2,1,0:T(8,128)S(1)} %fusion.29, bf16[1,2048,384]{2,1,0:T(8,128)(2,1)S(1)} %copy-done.7, bf16[32,1,24,384]{3,2,0,1:T(8,128)(2,1)S(1)} %copy-done.10), kind=kOutput, calls=%fused_computation.24 | convolution fusion | flops 1211105280 | bytes 11599872 | tf_op jit(solution)/shard_map/secf,edf->secd/dot_general | solution.py:91
  172.6 34.3 %all-to-all-done.2 = bf16[32,24,2048]{2,1,0:T(8,128)(2,1)} async-done(((bf16[32,24,2048]{2,1,0:T(8,128)(2,1)}), bf16[32,24,2048]{2,1,0:T(8,128)(2,1)}, u32[]{:S(2)}, u32[]{:S(2)}) %all-to-all-start.2) | async-done | bytes 3145760 | tf_op jit(solution)/shard_map/all_to_all | solution.py:191
  206.9 4.8 %all-to-all-start.3 = ((bf16[32,24,2048]{2,1,0:T(8,128)(2,1)}), bf16[32,24,2048]{2,1,0:T(8,128)(2,1)}, u32[]{:S(2)}, u32[]{:S(2)}) async-start(bf16[32,24,2048]{2,1,0:T(8,128)(2,1)} %bitcast.194), calls=%async_computation.3 | async-start | bytes 6291456 | tf_op jit(solution)/shard_map/all_to_all | solution.py:198
  211.7 0.0 reduce-scatter.5.cloned.1.call-start
  211.8 4.6 %fusion.15 = bf16[1,384,2048]{2,1,0:T(8,128)(2,1)} fusion(bf16[32,1,24,2048]{3,2,0,1:T(8,128)(2,1)} %bitcast.4, bf16[32,1,24,384]{3,2,0,1:T(8,128)(2,1)} %get-tuple-element.17), kind=kOutput, calls=%fused_computation.29 | convolution fusion | flops 1208745984 | bytes 5308416 | tf_op jit(solution)/shard_map/secf,secd->efd/dot_general | solution.py:77
  216.4 5.2 %multiply_reduce_fusion = f32[256,2048]{1,0:T(8,128)} fusion(bf16[768,2048,1]{1,0,2:T(8,128)(2,1)} %bitcast.52, f32[256,2]{0,1:T(2,128)S(1)} %bitcast.206, s32[256,2]{0,1:T(2,128)S(1)} %copy.88), kind=kOutput, calls=%fused_computation.10 | convolution fusion | flops 1612578816 | bytes 5246976 | tf_op jit(solution)/shard_map/dot_general | solution.py:201
  221.7 32.0 %all-to-all-done.3 = bf16[32,24,2048]{2,1,0:T(8,128)(2,1)} async-done(((bf16[32,24,2048]{2,1,0:T(8,128)(2,1)}), bf16[32,24,2048]{2,1,0:T(8,128)(2,1)}, u32[]{:S(2)}, u32[]{:S(2)}) %all-to-all-start.3) | async-done | bytes 3145760 | tf_op jit(solution)/shard_map/all_to_all | solution.py:198
  253.7 3.8 %multiply_reduce_fusion.1 = (f32[256]{0:T(256)S(1)}, f32[256,2048]{1,0:T(8,128)S(1)}) fusion(f32[256,2048]{1,0:T(8,128)} %copy-done.1, f32[2048]{0:T(1024)S(1)} %copy-done.14, bf16[768,256]{1,0:T(8,128)(2,1)S(1)} %fusion.61, bf16[768,2048]{1,0:T(8,128)(2,1)} %bitcast.56), kind=kOutput, calls=%fused_computation.35 | convolution fusion | flops 806878976 | bytes 7742464 | tf_op jit(solution)/shard_map/dot_general | solution.py:209
  257.6 2.0 fusion.51
  259.6 1.8 fusion.91
  (54 shorter events, 0.3 us)
Async XLA Ops:
  7.2 137.7 %copy-start = (bf16[1,384,2048]{2,1,0:T(8,128)(2,1)S(1)}, bf16[1,384,2048]{2,1,0:T(8,128)(2,1)}, u32[]{:S(2)}) copy-start(bf16[1,384,2048]{2,1,0:T(8,128)(2,1)} %param.24) | copy-start | bytes 4718596
  7.2 10.5 %copy-start.15 = (s32[1,256,2]{1,2,0:T(2,128)S(1)}, s32[1,256,2]{1,2,0:T(2,128)}, u32[]{:S(2)}) copy-start(s32[1,256,2]{1,2,0:T(2,128)} %param.20) | copy-start | bytes 6148
  7.2 12.3 %copy-start.3 = (bf16[1,256,2048]{2,1,0:T(8,128)(2,1)S(1)}, bf16[1,256,2048]{2,1,0:T(8,128)(2,1)}, u32[]{:S(2)}) copy-start(bf16[1,256,2048]{2,1,0:T(8,128)(2,1)} %param.25) | copy-start | bytes 3145732
  7.2 78.6 %all-gather.2.cloned.1.call-start = ((), (), s32[]{:S(2)}) async-start(), calls=%async_computation.6 | async-start | bytes 4718592 | tf_op jit(solution)/shard_map/all_gather | solution.py:145
  11.4 37.1 %collective-permute-start = (bf16[2,256,256]{1,2,0:T(8,128)(2,1)S(1)}, bf16[2,256,256]{1,2,0:T(8,128)(2,1)}, u32[]{:S(2)}, u32[]{:S(2)}) collective-permute-start(bf16[2,256,256]{1,2,0:T(8,128)(2,1)S(1)} %pad_maximum_fusion.1), channel_id=1, source_target_pairs={{0,16},{8,24},{16,32},{24,40},{32,48},{40,56},{48,64},{56,72},{64,... | collective-permute-start | bytes 786440 | tf_op jit(solution)/shard_map/ppermute | solution.py:21
  15.5 35.4 %collective-permute-start.1 = (bf16[2,256,256]{1,2,0:T(8,128)(2,1)S(1)}, bf16[2,256,256]{1,2,0:T(8,128)(2,1)}, u32[]{:S(2)}, u32[]{:S(2)}) collective-permute-start(bf16[2,256,256]{1,2,0:T(8,128)(2,1)S(1)} %pad_maximum_fusion.1), channel_id=1, source_target_pairs={{0,8},{8,16},{16,24},{24,32},{32,40},{40,48},{48,56},{56,64},{64,7... | collective-permute-start | bytes 786440 | tf_op jit(solution)/shard_map/ppermute | solution.py:21
  24.2 6.1 %copy-start.16 = (f32[1,256,2]{1,2,0:T(2,128)S(1)}, f32[1,256,2]{1,2,0:T(2,128)}, u32[]{:S(2)}) copy-start(f32[1,256,2]{1,2,0:T(2,128)} %param.21) | copy-start | bytes 6148
  36.5 7.6 %copy-start.17 = (s32[1,32]{1,0:T(1,128)S(1)}, s32[1,32]{1,0:T(1,128)}, u32[]{:S(2)}) copy-start(s32[1,32]{1,0:T(1,128)} %param.16) | copy-start | bytes 388
  36.5 49.3 %all-to-all-start = ((bf16[32,24,2048]{2,1,0:T(8,128)(2,1)}), bf16[32,24,2048]{2,1,0:T(8,128)(2,1)}, u32[]{:S(2)}, u32[]{:S(2)}) async-start(bf16[32,24,2048]{2,1,0:T(8,128)(2,1)} %bitcast.195), calls=%async_computation | async-start | bytes 6291456 | tf_op jit(solution)/shard_map/all_to_all | solution.py:138
  43.8 215.8 %reduce-scatter.3.cloned.1.call-start = ((), (), s32[]{:S(2)}) async-start(), calls=%async_computation.7 | async-start | bytes 3538944 | tf_op jit(solution)/shard_map/reduce_scatter | solution.py:219
  52.0 10.2 %copy-start.13 = (bf16[1,256,256]{1,2,0:T(8,128)(2,1)S(1)}, bf16[1,256,256]{1,2,0:T(8,128)(2,1)}, u32[]{:S(2)}) copy-start(bf16[1,256,256]{1,2,0:T(8,128)(2,1)} %get-tuple-element.22) | copy-start | bytes 393220
  85.8 7.5 %collective-permute-start.2 = (bf16[1024,2048]{1,0:T(8,128)(2,1)}, bf16[1024,2048]{1,0:T(8,128)(2,1)}, u32[]{:S(2)}, u32[]{:S(2)}) collective-permute-start(bf16[1024,2048]{1,0:T(8,128)(2,1)} %all-gather.2.cloned.1.call-done), channel_id=1, source_target_pairs={{0,8},{8,0},{16,24},{24,16},{32,40},{40,32},{48,56},{56,48},{64,72... | collective-permute-start | bytes 12582920 | tf_op jit(solution)/shard_map/ppermute | solution.py:173
  86.4 6.9 %copy-start.8 = (bf16[1,256,2048]{2,1,0:T(8,128)(2,1)S(1)}, bf16[1,256,2048]{2,1,0:T(8,128)(2,1)}, u32[]{:S(2)}) copy-start(bf16[1,256,2048]{2,1,0:T(8,128)(2,1)} %param.17) | copy-start | bytes 3145732
  86.4 6.9 %copy-start.12 = (bf16[2,128,8,256]{3,1,2,0:T(8,128)(2,1)S(1)}, bf16[2,128,8,256]{3,1,2,0:T(8,128)(2,1)}, u32[]{:S(2)}) copy-start(bf16[2,128,8,256]{3,1,2,0:T(8,128)(2,1)} %fusion.36) | copy-start | bytes 3145732
  90.2 6.9 %copy-start.14 = (f32[2048]{0:T(1024)S(1)}, f32[2048]{0:T(1024)}, u32[]{:S(2)}) copy-start(f32[2048]{0:T(1024)} %param.19) | copy-start | bytes 24580
  97.0 1.4 copy-start.1
  98.4 42.8 %copy-start.5 = (bf16[1,2048,384]{2,1,0:T(8,128)(2,1)S(1)}, bf16[1,2048,384]{2,1,0:T(8,128)(2,1)}, u32[]{:S(2)}) copy-start(bf16[1,2048,384]{2,1,0:T(8,128)(2,1)} %param.22) | copy-start | bytes 4718596
  141.2 1.8 copy-start.6
  149.8 1.9 copy-start.11
  149.8 1.9 copy-start.9
  160.1 46.8 %all-to-all-start.2 = ((bf16[32,24,2048]{2,1,0:T(8,128)(2,1)}), bf16[32,24,2048]{2,1,0:T(8,128)(2,1)}, u32[]{:S(2)}, u32[]{:S(2)}) async-start(bf16[32,24,2048]{2,1,0:T(8,128)(2,1)} %convolution_convert_fusion), calls=%async_computation.2 | async-start | bytes 6291456 | tf_op jit(solution)/shard_map/all_to_all | solution.py:191
  165.2 3.8 %copy-start.7 = (bf16[1,2048,384]{2,1,0:T(8,128)(2,1)S(1)}, bf16[1,2048,384]{2,1,0:T(8,128)(2,1)}, u32[]{:S(2)}) copy-start(bf16[1,2048,384]{2,1,0:T(8,128)(2,1)} %param.23) | copy-start | bytes 4718596
  165.2 3.8 %copy-start.10 = (bf16[32,1,24,384]{3,2,0,1:T(8,128)(2,1)S(1)}, bf16[32,1,24,384]{3,2,0,1:T(8,128)(2,1)}, u32[]{:S(2)}) copy-start(bf16[32,1,24,384]{3,2,0,1:T(8,128)(2,1)} %copy-done.9) | copy-start | bytes 1769476
  206.9 46.8 %all-to-all-start.3 = ((bf16[32,24,2048]{2,1,0:T(8,128)(2,1)}), bf16[32,24,2048]{2,1,0:T(8,128)(2,1)}, u32[]{:S(2)}, u32[]{:S(2)}) async-start(bf16[32,24,2048]{2,1,0:T(8,128)(2,1)} %bitcast.194), calls=%async_computation.3 | async-start | bytes 6291456 | tf_op jit(solution)/shard_map/all_to_all | solution.py:198
  211.7 49.7 %reduce-scatter.5.cloned.1.call-start = ((), (), s32[]{:S(2)}) async-start(), calls=%async_computation.8 | async-start | bytes 1769472 | tf_op jit(solution)/shard_map/reduce_scatter | solution.py:225
  253.7 3.8 %copy-start.2 = (f32[256,2048]{1,0:T(8,128)S(1)}, f32[256,2048]{1,0:T(8,128)}, u32[]{:S(2)}) copy-start(f32[256,2048]{1,0:T(8,128)} %copy-done.1) | copy-start | bytes 6291460
  253.7 3.8 %copy-start.4 = (f32[256,2048]{1,0:T(8,128)S(1)}, f32[256,2048]{1,0:T(8,128)}, u32[]{:S(2)}) copy-start(f32[256,2048]{1,0:T(8,128)} %multiply_reduce_fusion) | copy-start | bytes 6291460
Sparse Core Ops, SparseCore 0:
  10.3 64.7 all-gather.1
  155.7 45.2 reduce-scatter.2
  216.6 42.4 reduce-scatter.4
where the time goes:
time: 269 us; the launch traced here: 268 us
  waiting for transfers between devices  86.4 us (32%)
  matrix products  69.1 us (26%)
  blocking collectives  42.8 us (16%)
  local copies, waits for them, and re-layouts  24.5 us (9%)
  starting transfers between devices  23.8 us (9%)
  between operations  14.2 us (5%)
  other arithmetic  7.13 us (3%)
    all_to_all x1, blocking collectives, body(): lax.all_to_all(outgoing, 'seq', split_axis=0, concat_axis=0, tiled=True)  42.8 us
    all_to_all x1, waiting for transfers between devices, body(): lax.all_to_all(expert_out.reshape(sent_shape), 'seq', split_axis=0, conca...  34.3 us
    all_to_all x1, waiting for transfers between devices, body(): lax.all_to_all(grad_inputs.reshape(sent_shape), 'seq', split_axis=0, conc...  32 us
    all_to_all x1, waiting for transfers between devices, body(): lax.all_to_all(grads_outgoing, 'seq', split_axis=0, concat_axis=0, tiled=...  16.9 us
    mul x3, local copies, waits for them, and re-layouts, body(): route_gates[0][:, :, None] * cotangent[0].astype(jnp.float32)[:, None, :]  10.6 us
    sub x1, matrix products, attend_block(): raised = jnp.exp(scores - row_max)  10.2 us
    all_to_all x1, starting transfers between devices, body(): lax.all_to_all(grads_outgoing, 'seq', split_axis=0, concat_axis=0, tiled=...  7.31 us
    dot_general x1, matrix products, attend_block(): jnp.einsum('kgrs,skd->rkgd', probs, values_all.reshape(-1, KV, HD), prefe...  6.73 us
  transfers between devices with their start and end apart: 9, of which 4 were waited for; matrix products, arithmetic and copies ran while one was open for 30% of the time, Pallas kernels for 0%

commit v1 on v0

--- a/solution.py
+++ b/solution.py
@@ -120,21 +120,22 @@
     position = seq_index * tokens
 
     targets = slot_targets(routes[0], experts_all, capacity)
-    route_select = (
-        targets[None, :] == jnp.arange(slots, dtype=jnp.int32)[:, None]
-    ).astype(jnp.bfloat16)
-    token_select = route_select.reshape(slots, tokens, TOP).sum(axis=2)
+    chosen = targets.reshape(tokens, TOP)
+    slot_ids = jnp.arange(slots, dtype=jnp.int32)[:, None]
+    route_selects = [
+        (chosen[:, r][None, :] == slot_ids).astype(jnp.bfloat16) for r in range(TOP)
+    ]
+    token_select = sum(route_selects[1:], route_selects[0])
     sent_shape = (seq_count, owned * capacity, width)
     owner_shape = (seq_count, owned, capacity, width)
 
-    slot_grad = (route_gates[0][:, :, None] * cotangent[0].astype(jnp.float32)[:, None, :]).astype(
-        jnp.bfloat16
-    )
-    grads_outgoing = (
-        jnp.dot(route_select, slot_grad.reshape(tokens * TOP, width), preferred_element_type=jnp.float32)
-        .astype(jnp.bfloat16)
-        .reshape(sent_shape)
-    )
+    wide_cot = cotangent[0].astype(jnp.float32)
+    grads_sum = None
+    for r in range(TOP):
+        slot_grad_r = (route_gates[0][:, r : r + 1] * wide_cot).astype(jnp.bfloat16)
+        part = jnp.dot(route_selects[r], slot_grad_r, preferred_element_type=jnp.float32)
+        grads_sum = part if grads_sum is None else grads_sum + part
+    grads_outgoing = grads_sum.astype(jnp.bfloat16).reshape(sent_shape)
     grads_arrived = lax.all_to_all(
         grads_outgoing, "seq", split_axis=0, concat_axis=0, tiled=True
     ).reshape(owner_shape)
@@ -188,6 +189,9 @@
         owner_shape
     )
     pre_gate, pre_up, hidden, expert_out = expert_forward(arrived, w_gate, w_up, w_down)
+    expert_out, arrived, grads_arrived, pre_gate, pre_up, hidden = lax.optimization_barrier(
+        (expert_out, arrived, grads_arrived, pre_gate, pre_up, hidden)
+    )
     returned = lax.all_to_all(
         expert_out.reshape(sent_shape), "seq", split_axis=0, concat_axis=0, tiled=True
     )
@@ -198,13 +202,17 @@
     grads_returned = lax.all_to_all(
         grad_inputs.reshape(sent_shape), "seq", split_axis=0, concat_axis=0, tiled=True
     )
-    expert_rows = lax.dot_general(
-        route_select,
-        returned.reshape(slots, width),
-        (((0,), (0,)), ((), ())),
-        preferred_element_type=jnp.float32,
-    ).reshape(tokens, TOP, width)
-    mixture = jnp.sum(route_gates[0][:, :, None] * expert_rows, axis=1)
+    returned_rows = returned.reshape(slots, width)
+    mixture = None
+    for r in range(TOP):
+        rows_r = lax.dot_general(
+            route_selects[r],
+            returned_rows,
+            (((0,), (0,)), ((), ())),
+            preferred_element_type=jnp.float32,
+        )
+        term = route_gates[0][:, r : r + 1] * rows_r
+        mixture = term if mixture is None else mixture + term
     layer_out = (stream + mixture).astype(jnp.bfloat16)
     grad_normalized = lax.dot_general(
         token_select,

time: 269 us -> 258 us (0.959)
  local copies, waits for them, and re-layouts: 24.5 us -> 11.1 us
  waiting for transfers between devices: 86.4 us -> 92.6 us
  matrix products: 69.1 us -> 63 us
  blocking collectives: 42.8 us -> 46.7 us
    mul x3 -> x0, local copies, waits for them, and re-layouts: 10.6 us -> none  [body(): route_gates[0][:, :, None] * cotangent[0].astype(jnp.float32)[:, None, :]]
    all_to_all x1, waiting for transfers between devices: 16.9 us -> 20.7 us  [body(): lax.all_to_all(grads_outgoing, 'seq', split_axis=0, concat_axis=0, tiled=...]
    all_to_all x1, blocking collectives: 42.8 us -> 46.7 us  [body(): lax.all_to_all(outgoing, 'seq', split_axis=0, concat_axis=0, tiled=True)]
    dot_general x2 -> x4, matrix products: 11 us -> 9.02 us  [the longest x2 5.18 us: body(): lax.dot_general(route_selects[r], returned_rows, (((0,), (0,)), ((), ()))...]
  transfers between devices with their start and end apart: 9 -> 9, of which waited for: 4 -> 5; matrix products, arithmetic and copies ran while one was open for 30% -> 22% of each run, Pallas kernels for 0% -> 0%
where the time goes in v1:
time: 258 us; the launch traced here: 257 us
  waiting for transfers between devices  92.6 us (36%)
  matrix products  63 us (24%)
  blocking collectives  46.7 us (18%)
  starting transfers between devices  22.8 us (9%)
  between operations  14.3 us (6%)
  local copies, waits for them, and re-layouts  11.1 us (4%)
  other arithmetic  6.65 us (3%)
    all_to_all x1, blocking collectives, body(): lax.all_to_all(outgoing, 'seq', split_axis=0, concat_axis=0, tiled=True)  46.7 us
    all_to_all x1, waiting for transfers between devices, body(): lax.all_to_all(expert_out.reshape(sent_shape), 'seq', split_axis=0, conca...  34.6 us
    all_to_all x1, waiting for transfers between devices, body(): lax.all_to_all(grad_inputs.reshape(sent_shape), 'seq', split_axis=0, conc...  31.7 us
    all_to_all x1, waiting for transfers between devices, body(): lax.all_to_all(grads_outgoing, 'seq', split_axis=0, concat_axis=0, tiled=...  20.7 us
    sub x1, matrix products, attend_block(): raised = jnp.exp(scores - row_max)  10 us
    all_to_all x1, starting transfers between devices, body(): lax.all_to_all(grads_outgoing, 'seq', split_axis=0, concat_axis=0, tiled=...  7.31 us
    ppermute x2, starting transfers between devices, from_behind(): return lax.ppermute(shard, axis, pairs)  6.24 us
    dot_general x1, matrix products, attend_block(): jnp.einsum('kgrs,skd->rkgd', probs, values_all.reshape(-1, KV, HD), prefe...  5.7 us
  transfers between devices with their start and end apart: 9, of which 5 were waited for; matrix products, arithmetic and copies ran while one was open for 22% of the time, Pallas kernels for 0%

profile of v1, /device:TPU:32, one launch (start us, length us, event | category | flops | bytes accessed | tf_op | source)
XLA Modules:
  0.0 257.1 jit_solution(14592349571299432466)
XLA Ops:
  7.2 0.0 all-gather.2.cloned.1.call-start
  7.3 2.0 constant_dynamic-slice_fusion
  9.3 0.0 all-gather.2.cloned.1.call-update
  9.3 1.0 copy.72
  10.3 1.0 copy.73
  11.4 4.1 %collective-permute-start = (bf16[2,256,256]{1,2,0:T(8,128)(2,1)S(1)}, bf16[2,256,256]{1,2,0:T(8,128)(2,1)}, u32[]{:S(2)}, u32[]{:S(2)}) collective-permute-start(bf16[2,256,256]{1,2,0:T(8,128)(2,1)S(1)} %pad_maximum_fusion.1), channel_id=1, source_target_pairs={{0,16},{8,24},{16,32},{24,40},{32,48},{40,56},{48,64},{56,72},{64,... | collective-permute-start | bytes 786440 | tf_op jit(solution)/shard_map/ppermute | solution.py:21
  15.5 2.1 collective-permute-start.1
  17.6 0.1 copy.68
  17.8 0.1 eq.74
  17.9 0.1 eq.70
  18.1 1.2 reduce-window.18
  19.2 0.2 slice_reduce_fusion.2
  19.5 0.1 fusion.109
  19.6 0.1 reduce_sum.65
  19.8 0.2 slice_reduce_fusion
  20.1 1.1 fusion.66
  21.1 2.8 %add_convert_fusion.1 = bf16[768,2048]{1,0:T(8,128)(2,1)} fusion(f32[768,2048]{1,0:T(8,128)S(1)} %fusion.66, bf16[1,256,2048]{2,1,0:T(8,128)(2,1)S(1)} %copy-done.7, f32[256]{0:T(256)S(1)} %bitcast.235, s32[256]{0:T(256)S(1)} %get-tuple-element.27), kind=kOutput, calls=%fused_computation.8 | convolution fusion | flops 810221568 | bytes 10487808 | tf_op jit(solution)/shard_map/dot_general | solution.py:136
  23.9 7.3 %all-to-all-start = ((bf16[32,24,2048]{2,1,0:T(8,128)(2,1)}), bf16[32,24,2048]{2,1,0:T(8,128)(2,1)}, u32[]{:S(2)}, u32[]{:S(2)}) async-start(bf16[32,24,2048]{2,1,0:T(8,128)(2,1)} %bitcast.219), calls=%async_computation | async-start | bytes 6291456 | tf_op jit(solution)/shard_map/all_to_all | solution.py:139
  31.2 0.0 reduce-scatter.3.cloned.1.call-start
  31.3 0.1 copy.75
  31.4 0.1 reduce-window.20
  31.4 0.1 reduce.3
  31.6 0.1 convert_reduce_fusion.1
  31.7 0.1 convert_reduce_fusion
  31.8 1.4 and_and_fusion
  33.1 0.1 copy.79
  33.3 1.2 copy.86
  34.5 1.0 fusion.122
  35.5 0.1 copy.77
  35.6 1.0 fusion.123
  36.6 0.1 copy.78
  36.7 10.0 %fusion.125 = (f32[2,8,256]{2,1,0:T(8,128)S(1)}, f32[2,8,256,768]{2,3,1,0:T(8,128)}) fusion(pred[256,768]{0,1:T(8,128)(4,1)S(1)} %copy-done.17, bf16[256,2,8,128]{3,2,1,0:T(8,128)(2,1)} %bitcast.227, bf16[256,2,128]{2,0,1:T(8,128)(2,1)S(1)} %copy.79, bf16[256,2,128]{2,0,1:T(8,128)(2,1)S(1)} %copy.78, bf16[256,2,128]{2,0,1:T(8,128)(2,1)S(1)} %copy.77), kind=kOutput, calls=%fused_computation.142 | convolution fusion | flops 819069696 | bytes 14237696 | tf_op jit(solution)/shard_map/sub | solution.py:58
  46.8 5.7 %fusion.50 = bf16[2,128,8,256]{3,1,2,0:T(8,128)(2,1)S(1)} fusion(f32[2,8,256,768]{2,3,1,0:T(8,128)} %get-tuple-element.40, f32[2,8,256]{2,1,0:T(8,128)S(1)} %get-tuple-element.39, bf16[256,2,128]{0,2,1:T(8,128)(2,1)S(1)} %bitcast.228, bf16[256,2,128]{0,2,1:T(8,128)(2,1)S(1)} %bitcast.234, bf16[256,2,128]{0,2,1:T(8,128)(2,1)S(1)} %bitcast.233), kind=kOutput, calls=%fused_computation.60 | convolution fusion | flops 813301760 | bytes 14041088 | tf_op jit(solution)/shard_map/kgrs,skd->rkgd/dot_general | solution.py:60
  52.5 20.7 %all-to-all-done = bf16[32,24,2048]{2,1,0:T(8,128)(2,1)} async-done(((bf16[32,24,2048]{2,1,0:T(8,128)(2,1)}), bf16[32,24,2048]{2,1,0:T(8,128)(2,1)}, u32[]{:S(2)}, u32[]{:S(2)}) %all-to-all-start) | async-done | bytes 3145760 | tf_op jit(solution)/shard_map/all_to_all | solution.py:139
  73.2 1.6 all-gather.2.cloned.1.call-done
  74.8 3.5 %fusion.90 = f32[256,2048]{1,0:T(8,128)S(1)} fusion(bf16[1024,2048]{1,0:T(8,128)(2,1)} %all-gather.2.cloned.1.call-done, bf16[256,2048]{0,1:T(8,128)(2,1)S(1)} %bitcast.231, s32[]{:T(128)S(6)} %select_n.19), kind=kOutput, calls=%fused_computation.92 | convolution fusion | flops 1073741824 | bytes 6815748 | tf_op jit(solution)/shard_map/dot_general | solution.py:178
  78.3 3.9 %collective-permute-done.2 = bf16[1024,2048]{1,0:T(8,128)(2,1)} collective-permute-done((bf16[1024,2048]{1,0:T(8,128)(2,1)}, bf16[1024,2048]{1,0:T(8,128)(2,1)}, u32[]{:S(2)}, u32[]{:S(2)}) %collective-permute-start.2) | collective-permute-done | bytes 4194336 | tf_op jit(solution)/shard_map/ppermute | solution.py:174
  82.3 3.7 %multiply_reduce_fusion.1 = (f32[256]{0:T(256)S(1)}, f32[256,2048]{1,0:T(8,128)S(1)}) fusion(f32[256,2048]{1,0:T(8,128)S(1)} %fusion.90, bf16[1024,2048]{1,0:T(8,128)(2,1)} %collective-permute-done.2, bf16[256,2048]{0,1:T(8,128)(2,1)S(1)} %bitcast.232, s32[]{:T(128)S(6)} %select_n.21, bf16[1,256,2048]{2,1,0:T(8,128)(2,1)S(1)} %copy-done.13), kind=kOutput, calls=%fused_computation.50 | convolution fusion | flops 1077411584 | bytes 9962500 | tf_op jit(solution)/shard_map/dot_general | solution.py:179
  86.0 1.1 convolution_convert_fusion.1
  87.2 0.2 copy-done.2
  87.3 46.7 %all_to_all.20 = bf16[32,24,2048]{2,1,0:T(8,128)(2,1)S(1)} all-to-all(bf16[32,24,2048]{2,1,0:T(8,128)(2,1)S(1)} %bitcast.221), channel_id=1, replica_groups=mesh['seq'=32,'dp'=8] {'seq'}, dimensions={0} | all-to-all | bytes 6291456 | tf_op jit(solution)/shard_map/all_to_all | solution.py:188
  134.0 1.8 fusion.51
  135.8 1.9 multiply_convert_fusion.3
  137.8 3.5 %fusion.14 = bf16[32,1,24,2048]{3,2,0,1:T(8,128)(2,1)} fusion(bf16[1,384,2048]{2,1,0:T(8,128)(2,1)S(1)} %copy-done, bf16[32,1,24,384]{3,2,0,1:T(8,128)(2,1)S(1)} %get-tuple-element.26), kind=kOutput, calls=%fused_computation.29 | convolution fusion | flops 1209532416 | bytes 5308416 | tf_op jit(solution)/shard_map/secf,efd->secd/dot_general | solution.py:70
  141.3 4.0 %multiply_convert_fusion.1 = (bf16[32,1,24,384]{3,2,0,1:T(8,128)(2,1)S(1)}, bf16[32,1,24,384]{3,2,0,1:T(8,128)(2,1)S(1)}) fusion(f32[32,1,24,384]{3,2,0,1:T(8,128)S(1)} %fusion.51, f32[32,1,24,384]{3,2,0,1:T(8,128)S(1)} %get-tuple-element.21, bf16[1,384,2048]{2,1,0:T(8,128)(2,1)S(1)} %copy-done, bf16[32,1,24,2048]{3,2,0,1:T(8,128)(2,1)} %bitcast.9), kind=kOutput, calls=%fused_computation.65 | convolution fusion | flops 1211793408 | bytes 8257536 | tf_op jit(solution)/shard_map/secd,efd->secf/dot_general | solution.py:78
  145.3 1.9 fusion.24
  147.2 1.9 fusion.27
  149.1 2.0 pad_maximum_fusion
  151.1 0.0 reduce-scatter.3.cloned.1.call-update
  151.1 4.3 %all-to-all-start.2 = ((bf16[32,24,2048]{2,1,0:T(8,128)(2,1)}), bf16[32,24,2048]{2,1,0:T(8,128)(2,1)S(1)}, u32[]{:S(2)}, u32[]{:S(2)}) async-start(bf16[32,24,2048]{2,1,0:T(8,128)(2,1)} %bitcast.222), calls=%async_computation.2 | async-start | bytes 6291456 | tf_op jit(solution)/shard_map/all_to_all | solution.py:195
  155.4 3.6 %fusion.46 = f32[32,24,2048]{2,1,0:T(8,128)S(1)} fusion(bf16[1,2048,384]{2,1,0:T(8,128)(2,1)} %param.22, bf16[32,1,24,384]{3,2,0,1:T(8,128)(2,1)} %copy-done.16), kind=kOutput, calls=%fused_computation.56 | convolution fusion | flops 1207959552 | bytes 8454144 | tf_op jit(solution)/shard_map/secf,edf->secd/dot_general | solution.py:88
  159.0 3.5 %fusion.15 = bf16[32,1,24,2048]{3,2,0,1:T(8,128)(2,1)} fusion(f32[32,24,2048]{2,1,0:T(8,128)S(1)} %fusion.46, bf16[1,2048,384]{2,1,0:T(8,128)(2,1)S(1)} %copy-done.11, bf16[32,1,24,384]{3,2,0,1:T(8,128)(2,1)S(1)} %copy-done.15), kind=kOutput, calls=%fused_computation.30 | convolution fusion | flops 1211105280 | bytes 11599872 | tf_op jit(solution)/shard_map/secf,edf->secd/dot_general | solution.py:91
  162.6 34.6 %all-to-all-done.2 = bf16[32,24,2048]{2,1,0:T(8,128)(2,1)S(1)} async-done(((bf16[32,24,2048]{2,1,0:T(8,128)(2,1)}), bf16[32,24,2048]{2,1,0:T(8,128)(2,1)S(1)}, u32[]{:S(2)}, u32[]{:S(2)}) %all-to-all-start.2) | async-done | bytes 3145760 | tf_op jit(solution)/shard_map/all_to_all | solution.py:195
  197.2 4.8 %all-to-all-start.3 = ((bf16[32,24,2048]{2,1,0:T(8,128)(2,1)}), bf16[32,24,2048]{2,1,0:T(8,128)(2,1)}, u32[]{:S(2)}, u32[]{:S(2)}) async-start(bf16[32,24,2048]{2,1,0:T(8,128)(2,1)} %bitcast.220), calls=%async_computation.3 | async-start | bytes 6291456 | tf_op jit(solution)/shard_map/all_to_all | solution.py:202
  202.0 0.0 reduce-scatter.5.cloned.1.call-start
  202.1 4.7 %fusion.30 = bf16[1,384,2048]{2,1,0:T(8,128)(2,1)} fusion(bf16[32,1,24,2048]{3,2,0,1:T(8,128)(2,1)} %bitcast.9, bf16[32,1,24,384]{3,2,0,1:T(8,128)(2,1)} %copy-done.22), kind=kOutput, calls=%fused_computation.39 | convolution fusion | flops 1208745984 | bytes 5308416 | tf_op jit(solution)/shard_map/secf,secd->efd/dot_general | solution.py:77
  206.7 0.0 reduce-scatter.5.cloned.1.call-update
  206.8 3.1 %convolution_multiply_fusion.2 = f32[256,2048]{1,0:T(8,128)S(1)} fusion(bf16[768,2048]{1,0:T(8,128)(2,1)} %bitcast.217, f32[256]{0:T(256)S(1)} %bitcast.238, s32[256]{0:T(256)S(1)} %get-tuple-element.28), kind=kOutput, calls=%fused_computation.34 | convolution fusion | flops 806027264 | bytes 5244928 | tf_op jit(solution)/shard_map/dot_general | solution.py:208
  209.9 0.4 copy-done.6
  210.2 2.1 fusion.37
  212.4 31.7 %all-to-all-done.3 = bf16[32,24,2048]{2,1,0:T(8,128)(2,1)} async-done(((bf16[32,24,2048]{2,1,0:T(8,128)(2,1)}), bf16[32,24,2048]{2,1,0:T(8,128)(2,1)}, u32[]{:S(2)}, u32[]{:S(2)}) %all-to-all-start.3) | async-done | bytes 3145760 | tf_op jit(solution)/shard_map/all_to_all | solution.py:202
  244.0 3.2 %multiply_reduce_fusion = (f32[256]{0:T(256)S(1)}, f32[256,2048]{1,0:T(8,128)S(1)}) fusion(f32[256,2048]{1,0:T(8,128)S(1)} %copy-done.3, f32[2048]{0:T(1024)S(1)} %copy-done.18, bf16[768,2048]{1,0:T(8,128)(2,1)} %bitcast.59, s32[256]{0:T(256)S(1)} %get-tuple-element.27, s32[256]{0:T(256)S(1)} %get-tuple-element.28), kind=kOutput, calls=%fused_computation.48 | convolution fusion | flops 808451840 | bytes 7351296 | tf_op jit(solution)/shard_map/dot_general | solution.py:217
  247.3 1.5 fusion.64
  248.8 1.8 fusion.121
  (60 shorter events, 0.3 us)
Async XLA Ops:
  7.2 130.6 %copy-start = (bf16[1,384,2048]{2,1,0:T(8,128)(2,1)S(1)}, bf16[1,384,2048]{2,1,0:T(8,128)(2,1)}, u32[]{:S(2)}) copy-start(bf16[1,384,2048]{2,1,0:T(8,128)(2,1)} %param.24) | copy-start | bytes 4718596
  7.2 10.4 %copy-start.19 = (s32[1,256,2]{1,2,0:T(2,128)S(1)}, s32[1,256,2]{1,2,0:T(2,128)}, u32[]{:S(2)}) copy-start(s32[1,256,2]{1,2,0:T(2,128)} %param.20) | copy-start | bytes 6148
  7.2 67.6 %all-gather.2.cloned.1.call-start = ((), (), s32[]{:S(2)}) async-start(), calls=%async_computation.6 | async-start | bytes 4718592 | tf_op jit(solution)/shard_map/all_gather | solution.py:146
  7.2 12.8 %copy-start.20 = (f32[1,256,2]{1,2,0:T(2,128)S(1)}, f32[1,256,2]{1,2,0:T(2,128)}, u32[]{:S(2)}) copy-start(f32[1,256,2]{1,2,0:T(2,128)} %param.21) | copy-start | bytes 6148
  7.3 12.8 %copy-start.7 = (bf16[1,256,2048]{2,1,0:T(8,128)(2,1)S(1)}, bf16[1,256,2048]{2,1,0:T(8,128)(2,1)}, u32[]{:S(2)}) copy-start(bf16[1,256,2048]{2,1,0:T(8,128)(2,1)} %param.25) | copy-start | bytes 3145732
  11.4 23.1 %collective-permute-start = (bf16[2,256,256]{1,2,0:T(8,128)(2,1)S(1)}, bf16[2,256,256]{1,2,0:T(8,128)(2,1)}, u32[]{:S(2)}, u32[]{:S(2)}) collective-permute-start(bf16[2,256,256]{1,2,0:T(8,128)(2,1)S(1)} %pad_maximum_fusion.1), channel_id=1, source_target_pairs={{0,16},{8,24},{16,32},{24,40},{32,48},{40,56},{48,64},{56,72},{64,... | collective-permute-start | bytes 786440 | tf_op jit(solution)/shard_map/ppermute | solution.py:21
  15.5 20.1 %collective-permute-start.1 = (bf16[2,256,256]{1,2,0:T(8,128)(2,1)S(1)}, bf16[2,256,256]{1,2,0:T(8,128)(2,1)}, u32[]{:S(2)}, u32[]{:S(2)}) collective-permute-start(bf16[2,256,256]{1,2,0:T(8,128)(2,1)S(1)} %pad_maximum_fusion.1), channel_id=1, source_target_pairs={{0,8},{8,16},{16,24},{24,32},{32,40},{40,48},{48,56},{56,64},{64,7... | collective-permute-start | bytes 786440 | tf_op jit(solution)/shard_map/ppermute | solution.py:21
  23.9 7.4 %copy-start.21 = (s32[1,32]{1,0:T(1,128)S(1)}, s32[1,32]{1,0:T(1,128)}, u32[]{:S(2)}) copy-start(s32[1,32]{1,0:T(1,128)} %param.16) | copy-start | bytes 388
  23.9 9.4 %copy-start.12 = (bf16[1,256,2048]{2,1,0:T(8,128)(2,1)S(1)}, bf16[1,256,2048]{2,1,0:T(8,128)(2,1)}, u32[]{:S(2)}) copy-start(bf16[1,256,2048]{2,1,0:T(8,128)(2,1)} %param.13) | copy-start | bytes 3145732
  23.9 49.3 %all-to-all-start = ((bf16[32,24,2048]{2,1,0:T(8,128)(2,1)}), bf16[32,24,2048]{2,1,0:T(8,128)(2,1)}, u32[]{:S(2)}, u32[]{:S(2)}) async-start(bf16[32,24,2048]{2,1,0:T(8,128)(2,1)} %bitcast.219), calls=%async_computation | async-start | bytes 6291456 | tf_op jit(solution)/shard_map/all_to_all | solution.py:139
  31.2 217.6 %reduce-scatter.3.cloned.1.call-start = ((), (), s32[]{:S(2)}) async-start(), calls=%async_computation.7 | async-start | bytes 3538944 | tf_op jit(solution)/shard_map/reduce_scatter | solution.py:227
  33.3 3.5 %copy-start.17 = (pred[256,768]{0,1:T(8,128)(4,1)S(1)}, pred[256,768]{0,1:T(8,128)(4,1)}, u32[]{:S(2)}) copy-start(pred[256,768]{0,1:T(8,128)(4,1)} %and_and_fusion) | copy-start | bytes 589828
  74.8 7.5 %collective-permute-start.2 = (bf16[1024,2048]{1,0:T(8,128)(2,1)}, bf16[1024,2048]{1,0:T(8,128)(2,1)}, u32[]{:S(2)}, u32[]{:S(2)}) collective-permute-start(bf16[1024,2048]{1,0:T(8,128)(2,1)} %all-gather.2.cloned.1.call-done), channel_id=1, source_target_pairs={{0,8},{8,0},{16,24},{24,16},{32,40},{40,32},{48,56},{56,48},{64,72... | collective-permute-start | bytes 12582920 | tf_op jit(solution)/shard_map/ppermute | solution.py:174
  74.8 7.5 %copy-start.13 = (bf16[1,256,2048]{2,1,0:T(8,128)(2,1)S(1)}, bf16[1,256,2048]{2,1,0:T(8,128)(2,1)}, u32[]{:S(2)}) copy-start(bf16[1,256,2048]{2,1,0:T(8,128)(2,1)} %param.17) | copy-start | bytes 3145732
  78.3 7.7 %copy-start.18 = (f32[2048]{0:T(1024)S(1)}, f32[2048]{0:T(1024)}, u32[]{:S(2)}) copy-start(f32[2048]{0:T(1024)} %param.19) | copy-start | bytes 24580
  86.0 1.3 copy-start.2
  87.3 46.7 %copy-start.9 = (bf16[1,2048,384]{2,1,0:T(8,128)(2,1)S(1)}, bf16[1,2048,384]{2,1,0:T(8,128)(2,1)}, u32[]{:S(2)}) copy-start(bf16[1,2048,384]{2,1,0:T(8,128)(2,1)} %param.22) | copy-start | bytes 4718596
  134.0 1.8 copy-start.10
  137.7 3.5 %copy-start.22 = (bf16[32,1,24,384]{3,2,0,1:T(8,128)(2,1)}, bf16[32,1,24,384]{3,2,0,1:T(8,128)(2,1)S(1)}, u32[]{:S(2)}) copy-start(bf16[32,1,24,384]{3,2,0,1:T(8,128)(2,1)S(1)} %get-tuple-element.26) | copy-start | bytes 1769476
  145.3 1.9 copy-start.16
  145.3 1.9 copy-start.14
  151.1 46.1 %all-to-all-start.2 = ((bf16[32,24,2048]{2,1,0:T(8,128)(2,1)}), bf16[32,24,2048]{2,1,0:T(8,128)(2,1)S(1)}, u32[]{:S(2)}, u32[]{:S(2)}) async-start(bf16[32,24,2048]{2,1,0:T(8,128)(2,1)} %bitcast.222), calls=%async_computation.2 | async-start | bytes 6291456 | tf_op jit(solution)/shard_map/all_to_all | solution.py:195
  155.4 3.6 %copy-start.11 = (bf16[1,2048,384]{2,1,0:T(8,128)(2,1)S(1)}, bf16[1,2048,384]{2,1,0:T(8,128)(2,1)}, u32[]{:S(2)}) copy-start(bf16[1,2048,384]{2,1,0:T(8,128)(2,1)} %param.23) | copy-start | bytes 4718596
  155.4 3.6 %copy-start.15 = (bf16[32,1,24,384]{3,2,0,1:T(8,128)(2,1)S(1)}, bf16[32,1,24,384]{3,2,0,1:T(8,128)(2,1)}, u32[]{:S(2)}) copy-start(bf16[32,1,24,384]{3,2,0,1:T(8,128)(2,1)} %copy-done.14) | copy-start | bytes 1769476
  197.2 9.5 %copy-start.5 = (bf16[32,24,2048]{2,1,0:T(8,128)(2,1)}, bf16[32,24,2048]{2,1,0:T(8,128)(2,1)S(1)}, u32[]{:S(2)}) copy-start(bf16[32,24,2048]{2,1,0:T(8,128)(2,1)S(1)} %all-to-all-done.2) | copy-start | bytes 9437188
  197.2 46.8 %all-to-all-start.3 = ((bf16[32,24,2048]{2,1,0:T(8,128)(2,1)}), bf16[32,24,2048]{2,1,0:T(8,128)(2,1)}, u32[]{:S(2)}, u32[]{:S(2)}) async-start(bf16[32,24,2048]{2,1,0:T(8,128)(2,1)} %bitcast.220), calls=%async_computation.3 | async-start | bytes 6291456 | tf_op jit(solution)/shard_map/all_to_all | solution.py:202
  202.0 48.6 %reduce-scatter.5.cloned.1.call-start = ((), (), s32[]{:S(2)}) async-start(), calls=%async_computation.8 | async-start | bytes 1769472 | tf_op jit(solution)/shard_map/reduce_scatter | solution.py:233
  206.8 3.1 %copy-start.3 = (f32[256,2048]{1,0:T(8,128)S(1)}, f32[256,2048]{1,0:T(8,128)}, u32[]{:S(2)}) copy-start(f32[256,2048]{1,0:T(8,128)} %copy-done.2) | copy-start | bytes 6291460
  206.8 3.5 %copy-start.6 = (bf16[32,24,2048]{2,1,0:T(8,128)(2,1)S(1)}, bf16[32,24,2048]{2,1,0:T(8,128)(2,1)}, u32[]{:S(2)}) copy-start(bf16[32,24,2048]{2,1,0:T(8,128)(2,1)} %copy-done.5) | copy-start | bytes 9437188
  244.0 3.2 %copy-start.4 = (f32[256,2048]{1,0:T(8,128)S(1)}, f32[256,2048]{1,0:T(8,128)}, u32[]{:S(2)}) copy-start(f32[256,2048]{1,0:T(8,128)} %copy-done.2) | copy-start | bytes 6291460
  244.0 3.2 %copy-start.8 = (bf16[1,256,2048]{2,1,0:T(8,128)(2,1)S(1)}, bf16[1,256,2048]{2,1,0:T(8,128)(2,1)}, u32[]{:S(2)}) copy-start(bf16[1,256,2048]{2,1,0:T(8,128)(2,1)} %param.25) | copy-start | bytes 3145732
  247.2 3.4 %copy-start.1 = (bf16[1,384,2048]{2,1,0:T(8,128)(2,1)S(1)}, bf16[1,384,2048]{2,1,0:T(8,128)(2,1)}, u32[]{:S(2)}) copy-start(bf16[1,384,2048]{2,1,0:T(8,128)(2,1)} %param.24) | copy-start | bytes 4718596
Sparse Core Ops, SparseCore 0:
  10.3 64.4 all-gather.1
  151.2 41.9 reduce-scatter.2
  206.9 39.1 reduce-scatter.4

commit v2 on v1

--- a/solution.py
+++ b/solution.py
@@ -64,32 +64,30 @@
 
 
 def expert_forward(inputs, w_gate, w_up, w_down):
-    pre_gate = jnp.einsum("secd,edf->secf", inputs, w_gate, preferred_element_type=jnp.float32)
-    pre_up = jnp.einsum("secd,edf->secf", inputs, w_up, preferred_element_type=jnp.float32)
+    pre_gate = jnp.einsum("erd,edf->erf", inputs, w_gate, preferred_element_type=jnp.float32)
+    pre_up = jnp.einsum("erd,edf->erf", inputs, w_up, preferred_element_type=jnp.float32)
     hidden = (jax.nn.silu(pre_gate) * pre_up).astype(jnp.bfloat16)
     result = jnp.einsum(
-        "secf,efd->secd", hidden, w_down, preferred_element_type=jnp.float32
+        "erf,efd->erd", hidden, w_down, preferred_element_type=jnp.float32
     ).astype(jnp.bfloat16)
     return (pre_gate, pre_up, hidden, result)
 
 
 def expert_backward(inputs, grads_in, pre_gate, pre_up, hidden, w_gate, w_up, w_down):
-    grad_down = jnp.einsum("secf,secd->efd", hidden, grads_in, preferred_element_type=jnp.float32)
-    grad_hidden = jnp.einsum("secd,efd->secf", grads_in, w_down, preferred_element_type=jnp.float32)
+    grad_down = jnp.einsum("erf,erd->efd", hidden, grads_in, preferred_element_type=jnp.float32)
+    grad_hidden = jnp.einsum("erd,efd->erf", grads_in, w_down, preferred_element_type=jnp.float32)
     sigma = jax.nn.sigmoid(pre_gate)
     grad_pre_gate = (grad_hidden * pre_up * sigma * (1.0 + pre_gate * (1.0 - sigma))).astype(
         jnp.bfloat16
     )
     grad_pre_up = (grad_hidden * pre_gate * sigma).astype(jnp.bfloat16)
-    grad_gate = jnp.einsum(
-        "secd,secf->edf", inputs, grad_pre_gate, preferred_element_type=jnp.float32
-    )
-    grad_up = jnp.einsum("secd,secf->edf", inputs, grad_pre_up, preferred_element_type=jnp.float32)
+    grad_gate = jnp.einsum("erd,erf->edf", inputs, grad_pre_gate, preferred_element_type=jnp.float32)
+    grad_up = jnp.einsum("erd,erf->edf", inputs, grad_pre_up, preferred_element_type=jnp.float32)
     grad_inputs = jnp.einsum(
-        "secf,edf->secd", grad_pre_gate, w_gate, preferred_element_type=jnp.float32
+        "erf,edf->erd", grad_pre_gate, w_gate, preferred_element_type=jnp.float32
     )
     grad_inputs = grad_inputs + jnp.einsum(
-        "secf,edf->secd", grad_pre_up, w_up, preferred_element_type=jnp.float32
+        "erf,edf->erd", grad_pre_up, w_up, preferred_element_type=jnp.float32
     )
     return (grad_gate, grad_up, grad_down, grad_inputs.astype(jnp.bfloat16))
 
@@ -188,19 +186,30 @@
     arrived = lax.all_to_all(outgoing, "seq", split_axis=0, concat_axis=0, tiled=True).reshape(
         owner_shape
     )
+    rows_shape = (owned, seq_count * capacity, width)
+    arrived = arrived.transpose(1, 0, 2, 3).reshape(rows_shape)
+    grads_arrived = grads_arrived.transpose(1, 0, 2, 3).reshape(rows_shape)
     pre_gate, pre_up, hidden, expert_out = expert_forward(arrived, w_gate, w_up, w_down)
     expert_out, arrived, grads_arrived, pre_gate, pre_up, hidden = lax.optimization_barrier(
         (expert_out, arrived, grads_arrived, pre_gate, pre_up, hidden)
     )
     returned = lax.all_to_all(
-        expert_out.reshape(sent_shape), "seq", split_axis=0, concat_axis=0, tiled=True
+        expert_out.reshape(owned, seq_count, capacity, width).transpose(1, 0, 2, 3).reshape(sent_shape),
+        "seq",
+        split_axis=0,
+        concat_axis=0,
+        tiled=True,
     )
     grad_gate, grad_up, grad_down, grad_inputs = expert_backward(
         arrived, grads_arrived, pre_gate, pre_up, hidden, w_gate, w_up, w_down
     )
     returned, grad_inputs = lax.optimization_barrier((returned, grad_inputs))
     grads_returned = lax.all_to_all(
-        grad_inputs.reshape(sent_shape), "seq", split_axis=0, concat_axis=0, tiled=True
+        grad_inputs.reshape(owned, seq_count, capacity, width).transpose(1, 0, 2, 3).reshape(sent_shape),
+        "seq",
+        split_axis=0,
+        concat_axis=0,
+        tiled=True,
     )
     returned_rows = returned.reshape(slots, width)
     mixture = None

time: 258 us -> 259 us (level)
  waiting for transfers between devices: 92.6 us -> 87.6 us
  matrix products: 63 us -> 66.5 us
    all_to_all x1, waiting for transfers between devices: 20.7 us -> 17.1 us  [body(): lax.all_to_all(grads_outgoing, 'seq', split_axis=0, concat_axis=0, tiled=...]
  transfers between devices with their start and end apart: 9 -> 9, of which waited for: 5 -> 5; matrix products, arithmetic and copies ran while one was open for 22% -> 24% of each run, Pallas kernels for 0% -> 0%
where the time goes in v2:
time: 259 us
  waiting for transfers between devices  87.6 us (34%)
  matrix products  66.5 us (26%)
  blocking collectives  46.6 us (18%)
  starting transfers between devices  23.7 us (9%)
  between operations  14.2 us (5%)
  local copies, waits for them, and re-layouts  13.3 us (5%)
  other arithmetic  6.68 us (3%)
    all_to_all x1, blocking collectives, body(): lax.all_to_all(outgoing, 'seq', split_axis=0, concat_axis=0, tiled=True)  46.6 us
    all_to_all x1, waiting for transfers between devices, body(): lax.all_to_all(expert_out.reshape(owned, seq_count, capacity, width).tran...  34.8 us
    all_to_all x1, waiting for transfers between devices, body(): lax.all_to_all(grad_inputs.reshape(owned, seq_count, capacity, width).tra...  30.4 us
    all_to_all x1, waiting for transfers between devices, body(): lax.all_to_all(grads_outgoing, 'seq', split_axis=0, concat_axis=0, tiled=...  17.1 us
    sub x1, matrix products, attend_block(): raised = jnp.exp(scores - row_max)  10.2 us
    all_to_all x1, starting transfers between devices, body(): lax.all_to_all(grads_outgoing, 'seq', split_axis=0, concat_axis=0, tiled=...  7.3 us
    dot_general x2, matrix products, body(): lax.dot_general(route_selects[r], returned_rows, (((0,), (0,)), ((), ()))...  7.03 us
    dot_general x1, matrix products, attend_block(): jnp.einsum('kgrs,skd->rkgd', probs, values_all.reshape(-1, KV, HD), prefe...  6.66 us
  transfers between devices with their start and end apart: 9, of which 5 were waited for; matrix products, arithmetic and copies ran while one was open for 24% of the time, Pallas kernels for 0%

profile of v2, /device:TPU:32, one launch (start us, length us, event | category | flops | bytes accessed | tf_op | source)
XLA Modules:
  0.0 258.5 jit_solution(2237428321129975227)
XLA Ops:
  7.2 0.0 copy-start
  7.2 0.0 all-gather.2.cloned.1.call-start
  7.3 2.0 constant_dynamic-slice_fusion
  9.3 0.0 all-gather.2.cloned.1.call-update
  9.3 1.0 copy.56
  10.3 1.0 copy.57
  11.4 4.1 %collective-permute-start = (bf16[2,256,256]{1,2,0:T(8,128)(2,1)S(1)}, bf16[2,256,256]{1,2,0:T(8,128)(2,1)}, u32[]{:S(2)}, u32[]{:S(2)}) collective-permute-start(bf16[2,256,256]{1,2,0:T(8,128)(2,1)S(1)} %pad_maximum_fusion.1), channel_id=1, source_target_pairs={{0,16},{8,24},{16,32},{24,40},{32,48},{40,56},{48,64},{56,72},{64,... | collective-permute-start | bytes 786440 | tf_op jit(solution)/shard_map/ppermute | solution.py:21
  15.5 2.1 collective-permute-start.1
  17.6 0.1 copy.52
  17.8 0.1 eq.74
  17.9 0.1 eq.70
  18.1 1.2 reduce-window.18
  19.2 0.2 slice_reduce_fusion.2
  19.5 0.1 fusion.105
  19.6 0.1 reduce_sum.65
  19.8 0.2 slice_reduce_fusion
  20.1 1.1 fusion.63
  21.1 2.8 %add_convert_fusion.1 = bf16[768,2048]{1,0:T(8,128)(2,1)} fusion(f32[768,2048]{1,0:T(8,128)S(1)} %fusion.63, bf16[1,256,2048]{2,1,0:T(8,128)(2,1)S(1)} %copy-done.4, f32[256]{0:T(256)S(1)} %bitcast.195, s32[256]{0:T(256)S(1)} %get-tuple-element.27), kind=kOutput, calls=%fused_computation.8 | convolution fusion | flops 810221568 | bytes 10487808 | tf_op jit(solution)/shard_map/dot_general | solution.py:134
  23.9 7.3 %all-to-all-start = ((bf16[32,24,2048]{2,1,0:T(8,128)(2,1)}), bf16[32,24,2048]{2,1,0:T(8,128)(2,1)}, u32[]{:S(2)}, u32[]{:S(2)}) async-start(bf16[32,24,2048]{2,1,0:T(8,128)(2,1)} %bitcast.177), calls=%async_computation | async-start | bytes 6291456 | tf_op jit(solution)/shard_map/all_to_all | solution.py:137
  31.2 0.0 reduce-scatter.3.cloned.1.call-start
  31.3 0.1 copy.59
  31.4 0.1 reduce-window.20
  31.4 0.1 reduce.3
  31.6 0.1 convert_reduce_fusion.1
  31.7 0.1 convert_reduce_fusion
  31.8 1.4 and_and_fusion
  33.2 0.1 copy.63
  33.3 2.5 copy.70
  35.8 1.6 fusion.118
  37.4 0.8 copy.61
  38.2 1.0 fusion.119
  39.2 0.1 copy.62
  39.3 10.2 %fusion.121 = (f32[2,8,256]{2,1,0:T(8,128)S(1)}, f32[2,8,256,768]{2,3,1,0:T(8,128)}) fusion(pred[256,768]{0,1:T(8,128)(4,1)S(1)} %copy-done.12, bf16[256,2,8,128]{3,2,1,0:T(8,128)(2,1)} %bitcast.187, bf16[256,2,128]{2,0,1:T(8,128)(2,1)S(1)} %copy.63, bf16[256,2,128]{2,0,1:T(8,128)(2,1)S(1)} %copy.62, bf16[256,2,128]{2,0,1:T(8,128)(2,1)} %copy.61), kind=kOutput, calls=%fused_computation.139 | convolution fusion | flops 819069696 | bytes 14237696 | tf_op jit(solution)/shard_map/sub | solution.py:58
  49.5 6.7 %fusion.53 = bf16[2,128,8,256]{3,1,2,0:T(8,128)(2,1)} fusion(f32[2,8,256,768]{2,3,1,0:T(8,128)} %get-tuple-element.40, f32[2,8,256]{2,1,0:T(8,128)S(1)} %get-tuple-element.39, bf16[256,2,128]{0,2,1:T(8,128)(2,1)S(1)} %bitcast.188, bf16[256,2,128]{0,2,1:T(8,128)(2,1)S(1)} %bitcast.194, bf16[256,2,128]{0,2,1:T(8,128)(2,1)S(1)} %bitcast.193), kind=kOutput, calls=%fused_computation.60 | convolution fusion | flops 813301760 | bytes 14041088 | tf_op jit(solution)/shard_map/kgrs,skd->rkgd/dot_general | solution.py:60
  56.2 17.1 %all-to-all-done = bf16[32,24,2048]{2,1,0:T(8,128)(2,1)} async-done(((bf16[32,24,2048]{2,1,0:T(8,128)(2,1)}), bf16[32,24,2048]{2,1,0:T(8,128)(2,1)}, u32[]{:S(2)}, u32[]{:S(2)}) %all-to-all-start) | async-done | bytes 3145760 | tf_op jit(solution)/shard_map/all_to_all | solution.py:137
  73.2 1.5 all-gather.2.cloned.1.call-done
  74.8 3.8 %fusion.86 = f32[256,2048]{1,0:T(8,128)S(1)} fusion(bf16[1024,2048]{1,0:T(8,128)(2,1)} %all-gather.2.cloned.1.call-done, bf16[256,2048]{0,1:T(8,128)(2,1)} %bitcast.191, s32[]{:T(128)S(6)} %select_n.19), kind=kOutput, calls=%fused_computation.89 | convolution fusion | flops 1073741824 | bytes 6815748 | tf_op jit(solution)/shard_map/dot_general | solution.py:176
  78.6 3.7 %collective-permute-done.2 = bf16[1024,2048]{1,0:T(8,128)(2,1)} collective-permute-done((bf16[1024,2048]{1,0:T(8,128)(2,1)}, bf16[1024,2048]{1,0:T(8,128)(2,1)}, u32[]{:S(2)}, u32[]{:S(2)}) %collective-permute-start.2) | collective-permute-done | bytes 4194336 | tf_op jit(solution)/shard_map/ppermute | solution.py:172
  82.3 3.7 %multiply_reduce_fusion.1 = (f32[256]{0:T(256)S(1)}, f32[256,2048]{1,0:T(8,128)S(1)}) fusion(f32[256,2048]{1,0:T(8,128)S(1)} %fusion.86, bf16[1024,2048]{1,0:T(8,128)(2,1)} %collective-permute-done.2, bf16[256,2048]{0,1:T(8,128)(2,1)S(1)} %bitcast.192, s32[]{:T(128)S(6)} %select_n.21, bf16[1,256,2048]{2,1,0:T(8,128)(2,1)S(1)} %copy-done.8), kind=kOutput, calls=%fused_computation.50 | convolution fusion | flops 1077411584 | bytes 9962500 | tf_op jit(solution)/shard_map/dot_general | solution.py:177
  86.0 1.1 convolution_convert_fusion.1
  87.2 0.2 copy-done.1
  87.3 46.6 %all_to_all.20 = bf16[32,24,2048]{2,1,0:T(8,128)(2,1)S(1)} all-to-all(bf16[32,24,2048]{2,1,0:T(8,128)(2,1)S(1)} %bitcast.179), channel_id=1, replica_groups=mesh['seq'=32,'dp'=8] {'seq'}, dimensions={0} | all-to-all | bytes 6291456 | tf_op jit(solution)/shard_map/all_to_all | solution.py:186
  133.9 1.8 fusion.51
  135.7 1.9 multiply_convert_fusion.3
  137.6 3.4 %fusion.14 = bf16[1,768,2048]{2,1,0:T(8,128)(2,1)} fusion(bf16[768,384]{1,0:T(8,128)(2,1)S(1)} %get-tuple-element.43, bf16[1,384,2048]{2,1,0:T(8,128)(2,1)S(1)} %copy-done), kind=kOutput, calls=%fused_computation.26 | convolution fusion | flops 1209532416 | bytes 5308416 | tf_op jit(solution)/shard_map/erf,efd->erd/dot_general | solution.py:70
  141.1 4.0 %multiply_convert_fusion.1 = (bf16[1,768,384]{2,1,0:T(8,128)(2,1)S(1)}, bf16[1,768,384]{2,1,0:T(8,128)(2,1)S(1)}) fusion(f32[1,768,384]{2,1,0:T(8,128)S(1)} %bitcast.201, f32[1,768,384]{2,1,0:T(8,128)S(1)} %bitcast.202, bf16[1,384,2048]{2,1,0:T(8,128)(2,1)S(1)} %copy-done, bf16[1,768,2048]{2,1,0:T(8,128)(2,1)} %bitcast.31), kind=kOutput, calls=%fused_computation.63 | convolution fusion | flops 1211793408 | bytes 8257536 | tf_op jit(solution)/shard_map/erd,efd->erf/dot_general | solution.py:78
  145.1 1.9 fusion.30
  147.0 1.9 fusion.27
  148.9 2.0 pad_maximum_fusion
  150.9 0.0 reduce-scatter.3.cloned.1.call-update
  150.9 5.1 %all-to-all-start.2 = ((bf16[32,24,2048]{2,1,0:T(8,128)(2,1)}), bf16[32,24,2048]{2,1,0:T(8,128)(2,1)}, u32[]{:S(2)}, u32[]{:S(2)}) async-start(bf16[32,24,2048]{2,1,0:T(8,128)(2,1)} %bitcast.180), calls=%async_computation.2 | async-start | bytes 6291456 | tf_op jit(solution)/shard_map/all_to_all | solution.py:196
  156.0 3.4 %fusion.49 = f32[768,2048]{1,0:T(8,128)S(1)} fusion(bf16[1,2048,384]{2,1,0:T(8,128)(2,1)} %param.22, bf16[1,768,384]{2,1,0:T(8,128)(2,1)S(1)} %get-tuple-element.30), kind=kOutput, calls=%fused_computation.56 | convolution fusion | flops 1207959552 | bytes 8454144 | tf_op jit(solution)/shard_map/erf,edf->erd/dot_general | solution.py:86
  159.4 3.5 %fusion.15 = bf16[1,768,2048]{2,1,0:T(8,128)(2,1)} fusion(f32[768,2048]{1,0:T(8,128)S(1)} %fusion.49, bf16[1,2048,384]{2,1,0:T(8,128)(2,1)S(1)} %copy-done.7, bf16[1,768,384]{2,1,0:T(8,128)(2,1)S(1)} %copy-done.10), kind=kOutput, calls=%fused_computation.27 | convolution fusion | flops 1211105280 | bytes 11599872 | tf_op jit(solution)/shard_map/erf,edf->erd/dot_general | solution.py:89
  162.9 34.8 %all-to-all-done.2 = bf16[32,24,2048]{2,1,0:T(8,128)(2,1)} async-done(((bf16[32,24,2048]{2,1,0:T(8,128)(2,1)}), bf16[32,24,2048]{2,1,0:T(8,128)(2,1)}, u32[]{:S(2)}, u32[]{:S(2)}) %all-to-all-start.2) | async-done | bytes 3145760 | tf_op jit(solution)/shard_map/all_to_all | solution.py:196
  197.8 5.0 %all-to-all-start.3 = ((bf16[32,24,2048]{2,1,0:T(8,128)(2,1)}), bf16[32,24,2048]{2,1,0:T(8,128)(2,1)}, u32[]{:S(2)}, u32[]{:S(2)}) async-start(bf16[32,24,2048]{2,1,0:T(8,128)(2,1)} %bitcast.178), calls=%async_computation.3 | async-start | bytes 6291456 | tf_op jit(solution)/shard_map/all_to_all | solution.py:207
  202.7 0.0 reduce-scatter.5.cloned.1.call-start
  202.8 4.5 %fusion.33 = bf16[1,384,2048]{2,1,0:T(8,128)(2,1)} fusion(bf16[1,768,2048]{2,1,0:T(8,128)(2,1)} %bitcast.31, bf16[1,768,384]{2,1,0:T(8,128)(2,1)S(1)} %bitcast.203), kind=kOutput, calls=%fused_computation.39 | convolution fusion | flops 1208745984 | bytes 5308416 | tf_op jit(solution)/shard_map/erf,erd->efd/dot_general | solution.py:77
  207.3 0.0 reduce-scatter.5.cloned.1.call-update
  207.3 3.1 %convolution_multiply_fusion.2 = f32[256,2048]{1,0:T(8,128)S(1)} fusion(bf16[768,2048]{1,0:T(8,128)(2,1)} %bitcast.41, f32[256]{0:T(256)S(1)} %bitcast.198, s32[256]{0:T(256)S(1)} %get-tuple-element.28), kind=kOutput, calls=%fused_computation.34 | convolution fusion | flops 806027264 | bytes 5244928 | tf_op jit(solution)/shard_map/dot_general | solution.py:217
  210.4 4.0 %fusion.40 = bf16[1,256,2048]{2,1,0:T(8,128)(2,1)} fusion(f32[256,2048]{1,0:T(8,128)S(1)} %copy-done.2, f32[256,2048]{1,0:T(8,128)S(1)} %convolution_multiply_fusion.2, bf16[768,2048]{1,0:T(8,128)(2,1)} %bitcast.41, f32[256]{0:T(256)S(1)} %bitcast.196, s32[256]{0:T(256)S(1)} %get-tuple-element.27), kind=kOutput, calls=%fused_computation.44 | convolution fusion | flops 807600128 | bytes 8390656 | tf_op jit(solution)/shard_map/dot_general | solution.py:217
  214.4 30.4 %all-to-all-done.3 = bf16[32,24,2048]{2,1,0:T(8,128)(2,1)} async-done(((bf16[32,24,2048]{2,1,0:T(8,128)(2,1)}), bf16[32,24,2048]{2,1,0:T(8,128)(2,1)}, u32[]{:S(2)}, u32[]{:S(2)}) %all-to-all-start.3) | async-done | bytes 3145760 | tf_op jit(solution)/shard_map/all_to_all | solution.py:207
  244.7 3.9 %multiply_reduce_fusion = (f32[256]{0:T(256)S(1)}, f32[256,2048]{1,0:T(8,128)S(1)}) fusion(f32[256,2048]{1,0:T(8,128)} %copy-done.1, f32[2048]{0:T(1024)S(1)} %copy-done.14, bf16[768,2048]{1,0:T(8,128)(2,1)} %bitcast.44, s32[256]{0:T(256)S(1)} %get-tuple-element.27, s32[256]{0:T(256)S(1)} %get-tuple-element.28), kind=kOutput, calls=%fused_computation.48 | convolution fusion | flops 808451840 | bytes 7351296 | tf_op jit(solution)/shard_map/dot_general | solution.py:226
  248.6 1.5 fusion.61
  250.2 1.8 fusion.117
  (54 shorter events, 0.2 us)
Async XLA Ops:
  7.2 130.4 %copy-start = (bf16[1,384,2048]{2,1,0:T(8,128)(2,1)S(1)}, bf16[1,384,2048]{2,1,0:T(8,128)(2,1)}, u32[]{:S(2)}) copy-start(bf16[1,384,2048]{2,1,0:T(8,128)(2,1)} %param.24) | copy-start | bytes 4718596
  7.2 10.4 %copy-start.15 = (s32[1,256,2]{1,2,0:T(2,128)S(1)}, s32[1,256,2]{1,2,0:T(2,128)}, u32[]{:S(2)}) copy-start(s32[1,256,2]{1,2,0:T(2,128)} %param.20) | copy-start | bytes 6148
  7.2 67.6 %all-gather.2.cloned.1.call-start = ((), (), s32[]{:S(2)}) async-start(), calls=%async_computation.6 | async-start | bytes 4718592 | tf_op jit(solution)/shard_map/all_gather | solution.py:144
  7.2 12.8 %copy-start.16 = (f32[1,256,2]{1,2,0:T(2,128)S(1)}, f32[1,256,2]{1,2,0:T(2,128)}, u32[]{:S(2)}) copy-start(f32[1,256,2]{1,2,0:T(2,128)} %param.21) | copy-start | bytes 6148
  7.3 12.8 %copy-start.4 = (bf16[1,256,2048]{2,1,0:T(8,128)(2,1)S(1)}, bf16[1,256,2048]{2,1,0:T(8,128)(2,1)}, u32[]{:S(2)}) copy-start(bf16[1,256,2048]{2,1,0:T(8,128)(2,1)} %param.25) | copy-start | bytes 3145732
  11.4 24.4 %collective-permute-start = (bf16[2,256,256]{1,2,0:T(8,128)(2,1)S(1)}, bf16[2,256,256]{1,2,0:T(8,128)(2,1)}, u32[]{:S(2)}, u32[]{:S(2)}) collective-permute-start(bf16[2,256,256]{1,2,0:T(8,128)(2,1)S(1)} %pad_maximum_fusion.1), channel_id=1, source_target_pairs={{0,16},{8,24},{16,32},{24,40},{32,48},{40,56},{48,64},{56,72},{64,... | collective-permute-start | bytes 786440 | tf_op jit(solution)/shard_map/ppermute | solution.py:21
  15.5 22.7 %collective-permute-start.1 = (bf16[2,256,256]{1,2,0:T(8,128)(2,1)S(1)}, bf16[2,256,256]{1,2,0:T(8,128)(2,1)}, u32[]{:S(2)}, u32[]{:S(2)}) collective-permute-start(bf16[2,256,256]{1,2,0:T(8,128)(2,1)S(1)} %pad_maximum_fusion.1), channel_id=1, source_target_pairs={{0,8},{8,16},{16,24},{24,32},{32,40},{40,48},{48,56},{56,64},{64,7... | collective-permute-start | bytes 786440 | tf_op jit(solution)/shard_map/ppermute | solution.py:21
  23.9 7.4 %copy-start.17 = (s32[1,32]{1,0:T(1,128)S(1)}, s32[1,32]{1,0:T(1,128)}, u32[]{:S(2)}) copy-start(s32[1,32]{1,0:T(1,128)} %param.16) | copy-start | bytes 388
  23.9 49.3 %all-to-all-start = ((bf16[32,24,2048]{2,1,0:T(8,128)(2,1)}), bf16[32,24,2048]{2,1,0:T(8,128)(2,1)}, u32[]{:S(2)}, u32[]{:S(2)}) async-start(bf16[32,24,2048]{2,1,0:T(8,128)(2,1)} %bitcast.177), calls=%async_computation | async-start | bytes 6291456 | tf_op jit(solution)/shard_map/all_to_all | solution.py:137
  31.2 218.9 %reduce-scatter.3.cloned.1.call-start = ((), (), s32[]{:S(2)}) async-start(), calls=%async_computation.7 | async-start | bytes 3538944 | tf_op jit(solution)/shard_map/reduce_scatter | solution.py:236
  33.3 6.0 %copy-start.12 = (pred[256,768]{0,1:T(8,128)(4,1)S(1)}, pred[256,768]{0,1:T(8,128)(4,1)}, u32[]{:S(2)}) copy-start(pred[256,768]{0,1:T(8,128)(4,1)} %and_and_fusion) | copy-start | bytes 589828
  39.3 10.2 %copy-start.13 = (bf16[1,256,256]{1,2,0:T(8,128)(2,1)S(1)}, bf16[1,256,256]{1,2,0:T(8,128)(2,1)}, u32[]{:S(2)}) copy-start(bf16[1,256,256]{1,2,0:T(8,128)(2,1)} %get-tuple-element.33) | copy-start | bytes 393220
  74.8 7.5 %collective-permute-start.2 = (bf16[1024,2048]{1,0:T(8,128)(2,1)}, bf16[1024,2048]{1,0:T(8,128)(2,1)}, u32[]{:S(2)}, u32[]{:S(2)}) collective-permute-start(bf16[1024,2048]{1,0:T(8,128)(2,1)} %all-gather.2.cloned.1.call-done), channel_id=1, source_target_pairs={{0,8},{8,0},{16,24},{24,16},{32,40},{40,32},{48,56},{56,48},{64,72... | collective-permute-start | bytes 12582920 | tf_op jit(solution)/shard_map/ppermute | solution.py:172
  74.8 7.5 %copy-start.8 = (bf16[1,256,2048]{2,1,0:T(8,128)(2,1)S(1)}, bf16[1,256,2048]{2,1,0:T(8,128)(2,1)}, u32[]{:S(2)}) copy-start(bf16[1,256,2048]{2,1,0:T(8,128)(2,1)} %param.17) | copy-start | bytes 3145732
  74.8 7.5 %copy-start.11 = (bf16[2,128,8,256]{3,1,2,0:T(8,128)(2,1)S(1)}, bf16[2,128,8,256]{3,1,2,0:T(8,128)(2,1)}, u32[]{:S(2)}) copy-start(bf16[2,128,8,256]{3,1,2,0:T(8,128)(2,1)} %fusion.53) | copy-start | bytes 3145732
  78.5 7.5 %copy-start.14 = (f32[2048]{0:T(1024)S(1)}, f32[2048]{0:T(1024)}, u32[]{:S(2)}) copy-start(f32[2048]{0:T(1024)} %param.19) | copy-start | bytes 24580
  86.0 1.4 copy-start.1
  87.3 46.6 %copy-start.5 = (bf16[1,2048,384]{2,1,0:T(8,128)(2,1)S(1)}, bf16[1,2048,384]{2,1,0:T(8,128)(2,1)}, u32[]{:S(2)}) copy-start(bf16[1,2048,384]{2,1,0:T(8,128)(2,1)} %param.22) | copy-start | bytes 4718596
  133.9 1.8 copy-start.6
  137.6 3.5 %copy-start.18 = (bf16[768,384]{1,0:T(8,128)(2,1)}, bf16[768,384]{1,0:T(8,128)(2,1)S(1)}, u32[]{:S(2)}) copy-start(bf16[768,384]{1,0:T(8,128)(2,1)S(1)} %get-tuple-element.43) | copy-start | bytes 1769476
  145.1 1.9 copy-start.9
  150.9 46.8 %all-to-all-start.2 = ((bf16[32,24,2048]{2,1,0:T(8,128)(2,1)}), bf16[32,24,2048]{2,1,0:T(8,128)(2,1)}, u32[]{:S(2)}, u32[]{:S(2)}) async-start(bf16[32,24,2048]{2,1,0:T(8,128)(2,1)} %bitcast.180), calls=%async_computation.2 | async-start | bytes 6291456 | tf_op jit(solution)/shard_map/all_to_all | solution.py:196
  156.0 3.4 %copy-start.7 = (bf16[1,2048,384]{2,1,0:T(8,128)(2,1)S(1)}, bf16[1,2048,384]{2,1,0:T(8,128)(2,1)}, u32[]{:S(2)}) copy-start(bf16[1,2048,384]{2,1,0:T(8,128)(2,1)} %param.23) | copy-start | bytes 4718596
  156.0 3.4 %copy-start.10 = (bf16[1,768,384]{2,1,0:T(8,128)(2,1)S(1)}, bf16[1,768,384]{2,1,0:T(8,128)(2,1)}, u32[]{:S(2)}) copy-start(bf16[1,768,384]{2,1,0:T(8,128)(2,1)} %copy-done.9) | copy-start | bytes 1769476
  197.8 5.0 %copy-start.19 = (bf16[768,384]{1,0:T(8,128)(2,1)S(1)}, bf16[768,384]{1,0:T(8,128)(2,1)}, u32[]{:S(2)}) copy-start(bf16[768,384]{1,0:T(8,128)(2,1)} %copy-done.18) | copy-start | bytes 1769476
  197.8 47.0 %all-to-all-start.3 = ((bf16[32,24,2048]{2,1,0:T(8,128)(2,1)}), bf16[32,24,2048]{2,1,0:T(8,128)(2,1)}, u32[]{:S(2)}, u32[]{:S(2)}) async-start(bf16[32,24,2048]{2,1,0:T(8,128)(2,1)} %bitcast.178), calls=%async_computation.3 | async-start | bytes 6291456 | tf_op jit(solution)/shard_map/all_to_all | solution.py:207
  202.7 49.3 %reduce-scatter.5.cloned.1.call-start = ((), (), s32[]{:S(2)}) async-start(), calls=%async_computation.8 | async-start | bytes 1769472 | tf_op jit(solution)/shard_map/reduce_scatter | solution.py:242
  207.3 3.1 %copy-start.2 = (f32[256,2048]{1,0:T(8,128)S(1)}, f32[256,2048]{1,0:T(8,128)}, u32[]{:S(2)}) copy-start(f32[256,2048]{1,0:T(8,128)} %copy-done.1) | copy-start | bytes 6291460
  244.7 3.9 %copy-start.3 = (f32[256,2048]{1,0:T(8,128)S(1)}, f32[256,2048]{1,0:T(8,128)}, u32[]{:S(2)}) copy-start(f32[256,2048]{1,0:T(8,128)} %copy-done.1) | copy-start | bytes 6291460
Sparse Core Ops, SparseCore 0:
  10.3 64.4 all-gather.1
  151.0 41.9 reduce-scatter.2
  207.4 39.3 reduce-scatter.4

commit v3 on v1

--- a/solution.py
+++ b/solution.py
@@ -126,7 +126,11 @@
         (chosen[:, r][None, :] == slot_ids).astype(jnp.bfloat16) for r in range(TOP)
     ]
     token_select = sum(route_selects[1:], route_selects[0])
-    sent_shape = (seq_count, owned * capacity, width)
+    lanes = 128
+    if (owned * capacity * width) % (16 * lanes) == 0:
+        sent_shape = (seq_count, owned * capacity * width // lanes, lanes)
+    else:
+        sent_shape = (seq_count, owned * capacity, width)
     owner_shape = (seq_count, owned, capacity, width)
 
     wide_cot = cotangent[0].astype(jnp.float32)

time: 258 us -> 308 us (1.19)
  local copies, waits for them, and re-layouts: 11.1 us -> 61.8 us
  matrix products: 63 us -> 68.6 us
  waiting for transfers between devices: 92.6 us -> 87.5 us
    reshape x0 -> x8, local copies, waits for them, and re-layouts: none -> 41.8 us  [the longest x1 5.89 us: body(): grads_outgoing = grads_sum.astype(jnp.bfloat16).reshape(sent_shape)]
    another operation x2 -> x3, local copies, waits for them, and re-layouts: 0.09 us -> 6.02 us
    all_to_all x1, waiting for transfers between devices: 31.7 us -> 28.4 us  [body(): lax.all_to_all(grad_inputs.reshape(sent_shape), 'seq', split_axis=0, conc...]
    unnamed x50 -> x56, local copies, waits for them, and re-layouts: 3.98 us -> 7 us
  transfers between devices with their start and end apart: 9 -> 9, of which waited for: 5 -> 4; matrix products, arithmetic and copies ran while one was open for 22% -> 28% of each run, Pallas kernels for 0% -> 0%
where the time goes in v3:
time: 308 us; the launch traced here: 306 us
  waiting for transfers between devices  87.5 us (28%)
  matrix products  68.6 us (22%)
  local copies, waits for them, and re-layouts  61.8 us (20%)
  blocking collectives  44.5 us (14%)
  starting transfers between devices  22.8 us (7%)
  between operations  14.2 us (5%)
  other arithmetic  6.65 us (2%)
    all_to_all x1, blocking collectives, body(): lax.all_to_all(outgoing, 'seq', split_axis=0, concat_axis=0, tiled=True)  44.5 us
    all_to_all x1, waiting for transfers between devices, body(): lax.all_to_all(expert_out.reshape(sent_shape), 'seq', split_axis=0, conca...  34.4 us
    all_to_all x1, waiting for transfers between devices, body(): lax.all_to_all(grad_inputs.reshape(sent_shape), 'seq', split_axis=0, conc...  28.4 us
    all_to_all x1, waiting for transfers between devices, body(): lax.all_to_all(grads_outgoing, 'seq', split_axis=0, concat_axis=0, tiled=...  20.8 us
    sub x1, matrix products, attend_block(): raised = jnp.exp(scores - row_max)  10 us
    all_to_all x1, starting transfers between devices, body(): lax.all_to_all(grads_outgoing, 'seq', split_axis=0, concat_axis=0, tiled=...  7.29 us
    unnamed x56, local copies, waits for them, and re-layouts  7 us
    ppermute x2, starting transfers between devices, from_behind(): return lax.ppermute(shard, axis, pairs)  6.26 us
  transfers between devices with their start and end apart: 9, of which 4 were waited for; matrix products, arithmetic and copies ran while one was open for 28% of the time, Pallas kernels for 0%

profile of v3, /device:TPU:32, one launch (start us, length us, event | category | flops | bytes accessed | tf_op | source)
XLA Modules:
  0.0 306.1 jit_solution(11737442147395683674)
XLA Ops:
  7.3 2.0 constant_dynamic-slice_fusion
  9.3 1.0 copy.66
  10.3 1.0 copy.67
  11.4 4.1 %collective-permute-start = (bf16[2,256,256]{1,2,0:T(8,128)(2,1)S(1)}, bf16[2,256,256]{1,2,0:T(8,128)(2,1)}, u32[]{:S(2)}, u32[]{:S(2)}) collective-permute-start(bf16[2,256,256]{1,2,0:T(8,128)(2,1)S(1)} %pad_maximum_fusion.1), channel_id=1, source_target_pairs={{0,16},{8,24},{16,32},{24,40},{32,48},{40,56},{48,64},{56,72},{64,... | collective-permute-start | bytes 786440 | tf_op jit(solution)/shard_map/ppermute | solution.py:21
  15.5 2.2 collective-permute-start.1
  17.6 0.1 copy.62
  17.8 0.1 eq.74
  17.9 0.1 eq.70
  18.1 1.2 reduce-window.18
  19.3 0.2 slice_reduce_fusion.2
  19.5 0.1 fusion.109
  19.6 0.1 reduce_sum.65
  19.8 0.2 slice_reduce_fusion
  20.1 1.1 fusion.66
  21.1 2.7 add_convert_fusion.1
  23.9 5.9 %reshape.195 = bf16[32,384,128]{2,1,0:T(8,128)(2,1)} reshape(bf16[768,2048]{1,0:T(8,128)(2,1)} %add_convert_fusion.1) | data formatting | bytes 6291456 | tf_op jit(solution)/shard_map/reshape | solution.py:142
  29.8 7.3 %all-to-all-start = ((bf16[32,384,128]{2,1,0:T(8,128)(2,1)}), bf16[32,384,128]{2,1,0:T(8,128)(2,1)}, u32[]{:S(2)}, u32[]{:S(2)}) async-start(bf16[32,384,128]{2,1,0:T(8,128)(2,1)} %reshape.195), calls=%async_computation | async-start | bytes 6291456 | tf_op jit(solution)/shard_map/all_to_all | solution.py:143
  37.3 0.1 reduce.3
  37.4 0.1 convert_reduce_fusion.1
  37.6 1.4 and_and_fusion
  39.0 0.1 copy.73
  39.1 1.2 copy.80
  40.4 1.0 fusion.122
  41.3 0.1 copy.71
  41.5 1.0 fusion.123
  42.5 0.1 copy.72
  42.6 10.0 %fusion.125 = (f32[2,8,256]{2,1,0:T(8,128)S(1)}, f32[2,8,256,768]{2,3,1,0:T(8,128)}) fusion(pred[256,768]{0,1:T(8,128)(4,1)S(1)} %copy-done.19, bf16[256,2,8,128]{3,2,1,0:T(8,128)(2,1)} %bitcast.219, bf16[256,2,128]{2,0,1:T(8,128)(2,1)S(1)} %copy.73, bf16[256,2,128]{2,0,1:T(8,128)(2,1)S(1)} %copy.72, bf16[256,2,128]{2,0,1:T(8,128)(2,1)S(1)} %copy.71), kind=kOutput, calls=%fused_computation.142 | convolution fusion | flops 819069696 | bytes 14237696 | tf_op jit(solution)/shard_map/sub | solution.py:58
  52.6 5.7 %fusion.50 = bf16[2,128,8,256]{3,1,2,0:T(8,128)(2,1)S(1)} fusion(f32[2,8,256,768]{2,3,1,0:T(8,128)} %get-tuple-element.40, f32[2,8,256]{2,1,0:T(8,128)S(1)} %get-tuple-element.39, bf16[256,2,128]{0,2,1:T(8,128)(2,1)S(1)} %bitcast.220, bf16[256,2,128]{0,2,1:T(8,128)(2,1)S(1)} %bitcast.226, bf16[256,2,128]{0,2,1:T(8,128)(2,1)S(1)} %bitcast.225), kind=kOutput, calls=%fused_computation.60 | convolution fusion | flops 813301760 | bytes 14041088 | tf_op jit(solution)/shard_map/kgrs,skd->rkgd/dot_general | solution.py:60
  58.3 20.8 %all-to-all-done = bf16[32,384,128]{2,1,0:T(8,128)(2,1)} async-done(((bf16[32,384,128]{2,1,0:T(8,128)(2,1)}), bf16[32,384,128]{2,1,0:T(8,128)(2,1)}, u32[]{:S(2)}, u32[]{:S(2)}) %all-to-all-start) | async-done | bytes 3145760 | tf_op jit(solution)/shard_map/all_to_all | solution.py:143
  79.1 5.8 %reshape.196 = bf16[32,1,24,2048]{3,2,0,1:T(8,128)(2,1)} reshape(bf16[32,384,128]{2,1,0:T(8,128)(2,1)} %all-to-all-done) | data formatting | bytes 6291456 | tf_op jit(solution)/shard_map/reshape | solution.py:145
  84.9 3.5 %fusion.90 = f32[256,2048]{1,0:T(8,128)S(1)} fusion(bf16[1024,2048]{1,0:T(8,128)(2,1)} %all-gather.2.cloned.1.call-done, bf16[256,2048]{0,1:T(8,128)(2,1)S(1)} %bitcast.223, s32[]{:T(128)S(6)} %select_n.19), kind=kOutput, calls=%fused_computation.92 | convolution fusion | flops 1073741824 | bytes 6815748 | tf_op jit(solution)/shard_map/dot_general | solution.py:182
  88.5 3.9 %collective-permute-done.2 = bf16[1024,2048]{1,0:T(8,128)(2,1)} collective-permute-done((bf16[1024,2048]{1,0:T(8,128)(2,1)}, bf16[1024,2048]{1,0:T(8,128)(2,1)}, u32[]{:S(2)}, u32[]{:S(2)}) %collective-permute-start.2) | collective-permute-done | bytes 4194336 | tf_op jit(solution)/shard_map/ppermute | solution.py:178
  92.4 3.7 %multiply_reduce_fusion.1 = (f32[256]{0:T(256)S(1)}, f32[256,2048]{1,0:T(8,128)S(1)}) fusion(f32[256,2048]{1,0:T(8,128)S(1)} %fusion.90, bf16[1024,2048]{1,0:T(8,128)(2,1)} %collective-permute-done.2, bf16[256,2048]{0,1:T(8,128)(2,1)S(1)} %bitcast.224, s32[]{:T(128)S(6)} %select_n.21, bf16[1,256,2048]{2,1,0:T(8,128)(2,1)S(1)} %copy-done.15), kind=kOutput, calls=%fused_computation.50 | convolution fusion | flops 1077411584 | bytes 9962500 | tf_op jit(solution)/shard_map/dot_general | solution.py:183
  96.1 1.3 copy-done.2
  97.4 2.8 convolution_convert_fusion.1
  100.2 5.9 %reshape.199 = bf16[32,384,128]{2,1,0:T(8,128)(2,1)} reshape(bf16[768,2048]{1,0:T(8,128)(2,1)} %convolution_convert_fusion.1) | data formatting | bytes 6291456 | tf_op jit(solution)/shard_map/reshape | solution.py:190
  106.1 44.5 %all_to_all.20 = bf16[32,384,128]{2,1,0:T(8,128)(2,1)} all-to-all(bf16[32,384,128]{2,1,0:T(8,128)(2,1)} %reshape.199), channel_id=1, replica_groups=mesh['seq'=32,'dp'=8] {'seq'}, dimensions={0} | all-to-all | bytes 6291456 | tf_op jit(solution)/shard_map/all_to_all | solution.py:192
  150.6 5.9 %reshape.200 = bf16[32,24,2048]{2,1,0:T(8,128)(2,1)} reshape(bf16[32,384,128]{2,1,0:T(8,128)(2,1)} %all_to_all.20) | data formatting | bytes 6291456 | tf_op jit(solution)/shard_map/reshape.8
  156.5 3.9 %fusion.51 = f32[32,1,24,384]{3,2,0,1:T(8,128)S(1)} fusion(bf16[32,24,2048]{2,1,0:T(8,128)(2,1)} %reshape.200, bf16[1,2048,384]{2,1,0:T(8,128)(2,1)S(1)} %copy-done.11), kind=kOutput, calls=%fused_computation.61 | convolution fusion | flops 1207959552 | bytes 5898240 | tf_op jit(solution)/shard_map/secd,edf->secf/dot_general | solution.py:67
  160.4 2.8 multiply_convert_fusion.3
  163.3 3.5 %fusion.14 = bf16[32,1,24,2048]{3,2,0,1:T(8,128)(2,1)} fusion(bf16[1,384,2048]{2,1,0:T(8,128)(2,1)S(1)} %copy-done, bf16[32,1,24,384]{3,2,0,1:T(8,128)(2,1)S(1)} %get-tuple-element.26), kind=kOutput, calls=%fused_computation.29 | convolution fusion | flops 1209532416 | bytes 5308416 | tf_op jit(solution)/shard_map/secf,efd->secd/dot_general | solution.py:70
  166.8 5.8 %reshape.205 = bf16[32,1,24,2048]{3,2,0,1:T(8,128)(2,1)} reshape(bf16[32,384,128]{2,1,0:T(8,128)(2,1)} %all_to_all.20) | data formatting | bytes 6291456 | tf_op jit(solution)/shard_map/reshape | solution.py:192
  172.6 4.8 %multiply_convert_fusion.1 = (bf16[32,1,24,384]{3,2,0,1:T(8,128)(2,1)S(1)}, bf16[32,1,24,384]{3,2,0,1:T(8,128)(2,1)S(1)}) fusion(f32[32,1,24,384]{3,2,0,1:T(8,128)} %copy-done.25, f32[32,1,24,384]{3,2,0,1:T(8,128)} %get-tuple-element.21, bf16[1,384,2048]{2,1,0:T(8,128)(2,1)S(1)} %copy-done, bf16[32,1,24,2048]{3,2,0,1:T(8,128)(2,1)} %reshape.196), kind=kOutput, calls=%fused_computation.65 | convolution fusion | flops 1211793408 | bytes 8257536 | tf_op jit(solution)/shard_map/secd,efd->secf/dot_general | solution.py:78
  177.4 1.9 fusion.24
  179.3 1.9 fusion.27
  181.2 2.0 pad_maximum_fusion
  183.2 1.9 copy-done.8
  185.1 3.4 %reshape.206 = bf16[32,384,128]{2,1,0:T(8,128)(2,1)} reshape(bf16[32,1,24,2048]{3,2,0,1:T(8,128)(2,1)S(1)} %copy-done.8) | data formatting | bytes 6291456 | tf_op jit(solution)/shard_map/reshape | solution.py:200
  188.5 4.3 %all-to-all-start.2 = ((bf16[32,384,128]{2,1,0:T(8,128)(2,1)}), bf16[32,384,128]{2,1,0:T(8,128)(2,1)S(1)}, u32[]{:S(2)}, u32[]{:S(2)}) async-start(bf16[32,384,128]{2,1,0:T(8,128)(2,1)} %reshape.206), calls=%async_computation.2 | async-start | bytes 6291456 | tf_op jit(solution)/shard_map/all_to_all | solution.py:199
  192.8 3.8 %fusion.46 = f32[32,24,2048]{2,1,0:T(8,128)S(1)} fusion(bf16[1,2048,384]{2,1,0:T(8,128)(2,1)} %param.22, bf16[32,1,24,384]{3,2,0,1:T(8,128)(2,1)} %copy-done.18), kind=kOutput, calls=%fused_computation.56 | convolution fusion | flops 1207959552 | bytes 8454144 | tf_op jit(solution)/shard_map/secf,edf->secd/dot_general | solution.py:88
  196.6 3.6 %fusion.15 = bf16[32,1,24,2048]{3,2,0,1:T(8,128)(2,1)} fusion(f32[32,24,2048]{2,1,0:T(8,128)S(1)} %fusion.46, bf16[1,2048,384]{2,1,0:T(8,128)(2,1)S(1)} %copy-done.13, bf16[32,1,24,384]{3,2,0,1:T(8,128)(2,1)S(1)} %copy-done.17), kind=kOutput, calls=%fused_computation.30 | convolution fusion | flops 1211105280 | bytes 11599872 | tf_op jit(solution)/shard_map/secf,edf->secd/dot_general | solution.py:91
  200.2 34.4 %all-to-all-done.2 = bf16[32,384,128]{2,1,0:T(8,128)(2,1)S(1)} async-done(((bf16[32,384,128]{2,1,0:T(8,128)(2,1)}), bf16[32,384,128]{2,1,0:T(8,128)(2,1)S(1)}, u32[]{:S(2)}, u32[]{:S(2)}) %all-to-all-start.2) | async-done | bytes 3145760 | tf_op jit(solution)/shard_map/all_to_all | solution.py:199
  234.6 5.9 %reshape.211 = bf16[32,384,128]{2,1,0:T(8,128)(2,1)} reshape(bf16[32,1,24,2048]{3,2,0,1:T(8,128)(2,1)} %fusion.15) | data formatting | bytes 6291456 | tf_op jit(solution)/shard_map/reshape | solution.py:207
  240.4 4.8 %all-to-all-start.3 = ((bf16[32,384,128]{2,1,0:T(8,128)(2,1)}), bf16[32,384,128]{2,1,0:T(8,128)(2,1)}, u32[]{:S(2)}, u32[]{:S(2)}) async-start(bf16[32,384,128]{2,1,0:T(8,128)(2,1)} %reshape.211), calls=%async_computation.3 | async-start | bytes 6291456 | tf_op jit(solution)/shard_map/all_to_all | solution.py:206
  245.3 4.6 %fusion.30 = bf16[1,384,2048]{2,1,0:T(8,128)(2,1)} fusion(bf16[32,1,24,2048]{3,2,0,1:T(8,128)(2,1)} %reshape.196, bf16[32,1,24,384]{3,2,0,1:T(8,128)(2,1)} %copy-done.24), kind=kOutput, calls=%fused_computation.39 | convolution fusion | flops 1208745984 | bytes 5308416 | tf_op jit(solution)/shard_map/secf,secd->efd/dot_general | solution.py:77
  250.0 3.3 %reshape.210 = bf16[768,2048]{1,0:T(8,128)(2,1)} reshape(bf16[32,384,128]{2,1,0:T(8,128)(2,1)S(1)} %all-to-all-done.2) | data formatting | bytes 6291456 | tf_op jit(solution)/shard_map/reshape | solution.py:209
  253.3 3.1 %convolution_multiply_fusion.2 = f32[256,2048]{1,0:T(8,128)S(1)} fusion(bf16[768,2048]{1,0:T(8,128)(2,1)} %reshape.210, f32[256]{0:T(256)S(1)} %bitcast.230, s32[256]{0:T(256)S(1)} %get-tuple-element.28), kind=kOutput, calls=%fused_computation.34 | convolution fusion | flops 806027264 | bytes 5244928 | tf_op jit(solution)/shard_map/dot_general | solution.py:212
  256.4 0.4 copy-done.5
  256.8 2.1 fusion.37
  258.9 28.4 %all-to-all-done.3 = bf16[32,384,128]{2,1,0:T(8,128)(2,1)} async-done(((bf16[32,384,128]{2,1,0:T(8,128)(2,1)}), bf16[32,384,128]{2,1,0:T(8,128)(2,1)}, u32[]{:S(2)}, u32[]{:S(2)}) %all-to-all-start.3) | async-done | bytes 3145760 | tf_op jit(solution)/shard_map/all_to_all | solution.py:206
  287.3 5.8 %reshape.212 = bf16[768,2048]{1,0:T(8,128)(2,1)} reshape(bf16[32,384,128]{2,1,0:T(8,128)(2,1)} %all-to-all-done.3) | data formatting | bytes 6291456 | tf_op jit(solution)/shard_map/reshape | solution.py:223
  293.1 3.2 %multiply_reduce_fusion = (f32[256]{0:T(256)S(1)}, f32[256,2048]{1,0:T(8,128)S(1)}) fusion(f32[256,2048]{1,0:T(8,128)S(1)} %copy-done.3, f32[2048]{0:T(1024)S(1)} %copy-done.20, bf16[768,2048]{1,0:T(8,128)(2,1)} %reshape.212, s32[256]{0:T(256)S(1)} %get-tuple-element.27, s32[256]{0:T(256)S(1)} %get-tuple-element.28), kind=kOutput, calls=%fused_computation.48 | convolution fusion | flops 808451840 | bytes 7351296 | tf_op jit(solution)/shard_map/dot_general | solution.py:221
  296.3 1.5 fusion.64
  297.8 1.8 fusion.121
  (75 shorter events, 0.7 us)
Async XLA Ops:
  7.2 156.1 %copy-start = (bf16[1,384,2048]{2,1,0:T(8,128)(2,1)S(1)}, bf16[1,384,2048]{2,1,0:T(8,128)(2,1)}, u32[]{:S(2)}) copy-start(bf16[1,384,2048]{2,1,0:T(8,128)(2,1)} %param.24) | copy-start | bytes 4718596
  7.2 10.5 %copy-start.21 = (s32[1,256,2]{1,2,0:T(2,128)S(1)}, s32[1,256,2]{1,2,0:T(2,128)}, u32[]{:S(2)}) copy-start(s32[1,256,2]{1,2,0:T(2,128)} %param.20) | copy-start | bytes 6148
  7.2 77.7 %all-gather.2.cloned.1.call-start = ((), (), s32[]{:S(2)}) async-start(), calls=%async_computation.6 | async-start | bytes 4718592 | tf_op jit(solution)/shard_map/all_gather | solution.py:150
  7.2 12.8 %copy-start.22 = (f32[1,256,2]{1,2,0:T(2,128)S(1)}, f32[1,256,2]{1,2,0:T(2,128)}, u32[]{:S(2)}) copy-start(f32[1,256,2]{1,2,0:T(2,128)} %param.21) | copy-start | bytes 6148
  7.3 12.8 %copy-start.6 = (bf16[1,256,2048]{2,1,0:T(8,128)(2,1)S(1)}, bf16[1,256,2048]{2,1,0:T(8,128)(2,1)}, u32[]{:S(2)}) copy-start(bf16[1,256,2048]{2,1,0:T(8,128)(2,1)} %param.25) | copy-start | bytes 3145732
  11.4 29.0 %collective-permute-start = (bf16[2,256,256]{1,2,0:T(8,128)(2,1)S(1)}, bf16[2,256,256]{1,2,0:T(8,128)(2,1)}, u32[]{:S(2)}, u32[]{:S(2)}) collective-permute-start(bf16[2,256,256]{1,2,0:T(8,128)(2,1)S(1)} %pad_maximum_fusion.1), channel_id=1, source_target_pairs={{0,16},{8,24},{16,32},{24,40},{32,48},{40,56},{48,64},{56,72},{64,... | collective-permute-start | bytes 786440 | tf_op jit(solution)/shard_map/ppermute | solution.py:21
  15.5 26.0 %collective-permute-start.1 = (bf16[2,256,256]{1,2,0:T(8,128)(2,1)S(1)}, bf16[2,256,256]{1,2,0:T(8,128)(2,1)}, u32[]{:S(2)}, u32[]{:S(2)}) collective-permute-start(bf16[2,256,256]{1,2,0:T(8,128)(2,1)S(1)} %pad_maximum_fusion.1), channel_id=1, source_target_pairs={{0,8},{8,16},{16,24},{24,32},{32,40},{40,48},{48,56},{56,64},{64,7... | collective-permute-start | bytes 786440 | tf_op jit(solution)/shard_map/ppermute | solution.py:21
  29.8 7.4 %copy-start.23 = (s32[1,32]{1,0:T(1,128)S(1)}, s32[1,32]{1,0:T(1,128)}, u32[]{:S(2)}) copy-start(s32[1,32]{1,0:T(1,128)} %param.16) | copy-start | bytes 388
  29.8 9.4 %copy-start.14 = (bf16[1,256,2048]{2,1,0:T(8,128)(2,1)S(1)}, bf16[1,256,2048]{2,1,0:T(8,128)(2,1)}, u32[]{:S(2)}) copy-start(bf16[1,256,2048]{2,1,0:T(8,128)(2,1)} %param.13) | copy-start | bytes 3145732
  29.8 49.3 %all-to-all-start = ((bf16[32,384,128]{2,1,0:T(8,128)(2,1)}), bf16[32,384,128]{2,1,0:T(8,128)(2,1)}, u32[]{:S(2)}, u32[]{:S(2)}) async-start(bf16[32,384,128]{2,1,0:T(8,128)(2,1)} %reshape.195), calls=%async_computation | async-start | bytes 6291456 | tf_op jit(solution)/shard_map/all_to_all | solution.py:143
  37.1 260.7 %reduce-scatter.3.cloned.1.call-start = ((), (), s32[]{:S(2)}) async-start(), calls=%async_computation.7 | async-start | bytes 3538944 | tf_op jit(solution)/shard_map/reduce_scatter | solution.py:231
  39.1 3.5 %copy-start.19 = (pred[256,768]{0,1:T(8,128)(4,1)S(1)}, pred[256,768]{0,1:T(8,128)(4,1)}, u32[]{:S(2)}) copy-start(pred[256,768]{0,1:T(8,128)(4,1)} %and_and_fusion) | copy-start | bytes 589828
  84.9 7.5 %collective-permute-start.2 = (bf16[1024,2048]{1,0:T(8,128)(2,1)}, bf16[1024,2048]{1,0:T(8,128)(2,1)}, u32[]{:S(2)}, u32[]{:S(2)}) collective-permute-start(bf16[1024,2048]{1,0:T(8,128)(2,1)} %all-gather.2.cloned.1.call-done), channel_id=1, source_target_pairs={{0,8},{8,0},{16,24},{24,16},{32,40},{40,32},{48,56},{56,48},{64,72... | collective-permute-start | bytes 12582920 | tf_op jit(solution)/shard_map/ppermute | solution.py:178
  84.9 7.5 %copy-start.15 = (bf16[1,256,2048]{2,1,0:T(8,128)(2,1)S(1)}, bf16[1,256,2048]{2,1,0:T(8,128)(2,1)}, u32[]{:S(2)}) copy-start(bf16[1,256,2048]{2,1,0:T(8,128)(2,1)} %param.17) | copy-start | bytes 3145732
  88.5 9.0 %copy-start.20 = (f32[2048]{0:T(1024)S(1)}, f32[2048]{0:T(1024)}, u32[]{:S(2)}) copy-start(f32[2048]{0:T(1024)} %param.19) | copy-start | bytes 24580
  96.1 1.3 copy-start.2
  150.6 5.9 %copy-start.11 = (bf16[1,2048,384]{2,1,0:T(8,128)(2,1)S(1)}, bf16[1,2048,384]{2,1,0:T(8,128)(2,1)}, u32[]{:S(2)}) copy-start(bf16[1,2048,384]{2,1,0:T(8,128)(2,1)} %param.22) | copy-start | bytes 4718596
  156.5 3.9 %copy-start.10 = (bf16[32,24,2048]{2,1,0:T(8,128)(2,1)S(1)}, bf16[32,24,2048]{2,1,0:T(8,128)(2,1)}, u32[]{:S(2)}) copy-start(bf16[32,24,2048]{2,1,0:T(8,128)(2,1)} %reshape.200) | copy-start | bytes 9437188
  156.5 3.9 %copy-start.12 = (bf16[1,2048,384]{2,1,0:T(8,128)(2,1)S(1)}, bf16[1,2048,384]{2,1,0:T(8,128)(2,1)}, u32[]{:S(2)}) copy-start(bf16[1,2048,384]{2,1,0:T(8,128)(2,1)} %param.23) | copy-start | bytes 4718596
  160.4 2.9 copy-start.25
  163.3 3.5 %copy-start.24 = (bf16[32,1,24,384]{3,2,0,1:T(8,128)(2,1)}, bf16[32,1,24,384]{3,2,0,1:T(8,128)(2,1)S(1)}, u32[]{:S(2)}) copy-start(bf16[32,1,24,384]{3,2,0,1:T(8,128)(2,1)S(1)} %get-tuple-element.26) | copy-start | bytes 1769476
  172.5 4.8 %copy-start.9 = (bf16[32,1,24,2048]{3,2,0,1:T(8,128)(2,1)S(1)}, bf16[32,1,24,2048]{3,2,0,1:T(8,128)(2,1)}, u32[]{:S(2)}) copy-start(bf16[32,1,24,2048]{3,2,0,1:T(8,128)(2,1)} %reshape.205) | copy-start | bytes 9437188
  177.4 1.9 copy-start.18
  177.4 1.9 copy-start.16
  183.2 1.9 copy-start.8
  188.5 46.1 %all-to-all-start.2 = ((bf16[32,384,128]{2,1,0:T(8,128)(2,1)}), bf16[32,384,128]{2,1,0:T(8,128)(2,1)S(1)}, u32[]{:S(2)}, u32[]{:S(2)}) async-start(bf16[32,384,128]{2,1,0:T(8,128)(2,1)} %reshape.206), calls=%async_computation.2 | async-start | bytes 6291456 | tf_op jit(solution)/shard_map/all_to_all | solution.py:199
  192.8 3.8 %copy-start.13 = (bf16[1,2048,384]{2,1,0:T(8,128)(2,1)S(1)}, bf16[1,2048,384]{2,1,0:T(8,128)(2,1)}, u32[]{:S(2)}) copy-start(bf16[1,2048,384]{2,1,0:T(8,128)(2,1)} %param.23) | copy-start | bytes 4718596
  192.8 3.8 %copy-start.17 = (bf16[32,1,24,384]{3,2,0,1:T(8,128)(2,1)S(1)}, bf16[32,1,24,384]{3,2,0,1:T(8,128)(2,1)}, u32[]{:S(2)}) copy-start(bf16[32,1,24,384]{3,2,0,1:T(8,128)(2,1)} %copy-done.16) | copy-start | bytes 1769476
  240.4 46.8 %all-to-all-start.3 = ((bf16[32,384,128]{2,1,0:T(8,128)(2,1)}), bf16[32,384,128]{2,1,0:T(8,128)(2,1)}, u32[]{:S(2)}, u32[]{:S(2)}) async-start(bf16[32,384,128]{2,1,0:T(8,128)(2,1)} %reshape.211), calls=%async_computation.3 | async-start | bytes 6291456 | tf_op jit(solution)/shard_map/all_to_all | solution.py:206
  245.3 54.3 %reduce-scatter.5.cloned.1.call-start = ((), (), s32[]{:S(2)}) async-start(), calls=%async_computation.8 | async-start | bytes 1769472 | tf_op jit(solution)/shard_map/reduce_scatter | solution.py:237
  253.3 3.1 %copy-start.3 = (f32[256,2048]{1,0:T(8,128)S(1)}, f32[256,2048]{1,0:T(8,128)}, u32[]{:S(2)}) copy-start(f32[256,2048]{1,0:T(8,128)} %copy-done.2) | copy-start | bytes 6291460
  253.3 3.5 %copy-start.5 = (bf16[768,2048]{1,0:T(8,128)(2,1)S(1)}, bf16[768,2048]{1,0:T(8,128)(2,1)}, u32[]{:S(2)}) copy-start(bf16[768,2048]{1,0:T(8,128)(2,1)} %reshape.210) | copy-start | bytes 9437188
  293.1 3.2 %copy-start.4 = (f32[256,2048]{1,0:T(8,128)S(1)}, f32[256,2048]{1,0:T(8,128)}, u32[]{:S(2)}) copy-start(f32[256,2048]{1,0:T(8,128)} %copy-done.2) | copy-start | bytes 6291460
  293.1 3.2 %copy-start.7 = (bf16[1,256,2048]{2,1,0:T(8,128)(2,1)S(1)}, bf16[1,256,2048]{2,1,0:T(8,128)(2,1)}, u32[]{:S(2)}) copy-start(bf16[1,256,2048]{2,1,0:T(8,128)(2,1)} %param.25) | copy-start | bytes 3145732
  296.2 3.4 %copy-start.1 = (bf16[1,384,2048]{2,1,0:T(8,128)(2,1)S(1)}, bf16[1,384,2048]{2,1,0:T(8,128)(2,1)}, u32[]{:S(2)}) copy-start(bf16[1,384,2048]{2,1,0:T(8,128)(2,1)} %param.24) | copy-start | bytes 4718596
Sparse Core Ops, SparseCore 0:
  10.3 64.4 all-gather.1
  183.3 45.3 reduce-scatter.2
  250.1 42.4 reduce-scatter.4

commit v4 on v1

--- a/solution.py
+++ b/solution.py
@@ -189,19 +189,20 @@
         owner_shape
     )
     pre_gate, pre_up, hidden, expert_out = expert_forward(arrived, w_gate, w_up, w_down)
-    expert_out, arrived, grads_arrived, pre_gate, pre_up, hidden = lax.optimization_barrier(
-        (expert_out, arrived, grads_arrived, pre_gate, pre_up, hidden)
-    )
-    returned = lax.all_to_all(
-        expert_out.reshape(sent_shape), "seq", split_axis=0, concat_axis=0, tiled=True
-    )
     grad_gate, grad_up, grad_down, grad_inputs = expert_backward(
         arrived, grads_arrived, pre_gate, pre_up, hidden, w_gate, w_up, w_down
     )
-    returned, grad_inputs = lax.optimization_barrier((returned, grad_inputs))
-    grads_returned = lax.all_to_all(
-        grad_inputs.reshape(sent_shape), "seq", split_axis=0, concat_axis=0, tiled=True
-    )
+    both_back = lax.all_to_all(
+        jnp.concatenate(
+            [expert_out.reshape(sent_shape), grad_inputs.reshape(sent_shape)], axis=1
+        ),
+        "seq",
+        split_axis=0,
+        concat_axis=0,
+        tiled=True,
+    )
+    returned = both_back[:, : owned * capacity]
+    grads_returned = both_back[:, owned * capacity :]
     returned_rows = returned.reshape(slots, width)
     mixture = None
     for r in range(TOP):

time: 258 us -> 273 us (1.058)
  blocking collectives: 46.7 us -> 0 us
  waiting for transfers between devices: 92.6 us -> 132 us
  matrix products: 63 us -> 73.1 us
  local copies, waits for them, and re-layouts: 11.1 us -> 16.7 us
  other arithmetic: 6.65 us -> 10.4 us
  starting transfers between devices: 22.8 us -> 25.7 us
    all_to_all x1 -> x0, blocking collectives: 46.7 us -> none  [body(): lax.all_to_all(outgoing, 'seq', split_axis=0, concat_axis=0, tiled=True)]
    all_to_all x2, waiting for transfers between devices: 66.3 us -> 110 us  [the longest x1 73.3 us: body(): lax.all_to_all(jnp.concatenate([expert_out.reshape(sent_shape), grad_inpu...]
    concatenate x0 -> x1, other arithmetic: none -> 3.77 us  [body(): jnp.concatenate([expert_out.reshape(sent_shape), grad_inputs.reshape(sent...]
    all_to_all x1, waiting for transfers between devices: 20.7 us -> 17.2 us  [body(): lax.all_to_all(grads_outgoing, 'seq', split_axis=0, concat_axis=0, tiled=...]
    slice x1 -> x2, local copies, waits for them, and re-layouts: 0.22 us -> 3.79 us  [the longest x1 3.57 us: body(): grads_returned = both_back[:, owned * capacity:]]
    dot_general x1, matrix products: 1.89 us -> 5.09 us  [expert_forward(): jnp.einsum('secd,edf->secf', inputs, w_up, preferred_element_type=jnp.flo...]
    all_to_all x2, starting transfers between devices: 9.12 us -> 12 us  [the longest x1 7.02 us: body(): lax.all_to_all(outgoing, 'seq', split_axis=0, concat_axis=0, tiled=True)]
  transfers between devices with their start and end apart: 9 -> 9, of which waited for: 5 -> 5; matrix products, arithmetic and copies ran while one was open for 22% -> 25% of each run, Pallas kernels for 0% -> 0%
where the time goes in v4:
time: 273 us
  waiting for transfers between devices  132 us (48%)
  matrix products  73.1 us (27%)
  starting transfers between devices  25.7 us (9%)
  local copies, waits for them, and re-layouts  16.7 us (6%)
  between operations  14.2 us (5%)
  other arithmetic  10.4 us (4%)
    all_to_all x1, waiting for transfers between devices, body(): lax.all_to_all(jnp.concatenate([expert_out.reshape(sent_shape), grad_inpu...  73.3 us
    all_to_all x1, waiting for transfers between devices, body(): lax.all_to_all(outgoing, 'seq', split_axis=0, concat_axis=0, tiled=True)  36.7 us
    all_to_all x1, waiting for transfers between devices, body(): lax.all_to_all(grads_outgoing, 'seq', split_axis=0, concat_axis=0, tiled=...  17.2 us
    sub x1, matrix products, attend_block(): raised = jnp.exp(scores - row_max)  10.1 us
    all_to_all x1, starting transfers between devices, body(): lax.all_to_all(grads_outgoing, 'seq', split_axis=0, concat_axis=0, tiled=...  7.26 us
    all_to_all x1, starting transfers between devices, body(): lax.all_to_all(outgoing, 'seq', split_axis=0, concat_axis=0, tiled=True)  7.02 us
    dot_general x1, matrix products, attend_block(): jnp.einsum('kgrs,skd->rkgd', probs, values_all.reshape(-1, KV, HD), prefe...  6.67 us
    ppermute x2, starting transfers between devices, from_behind(): return lax.ppermute(shard, axis, pairs)  6.29 us
  transfers between devices with their start and end apart: 9, of which 5 were waited for; matrix products, arithmetic and copies ran while one was open for 25% of the time, Pallas kernels for 0%

profile of v4, /device:TPU:32, one launch (start us, length us, event | category | flops | bytes accessed | tf_op | source)
XLA Modules:
  0.0 272.6 jit_solution(3653122003241215253)
XLA Ops:
  7.2 0.0 copy-start
  7.2 0.0 all-gather.2.cloned.1.call-start
  7.3 2.0 constant_dynamic-slice_fusion
  9.3 0.0 all-gather.2.cloned.1.call-update
  9.3 1.0 copy.72
  10.3 1.0 copy.73
  11.4 4.1 %collective-permute-start = (bf16[2,256,256]{1,2,0:T(8,128)(2,1)S(1)}, bf16[2,256,256]{1,2,0:T(8,128)(2,1)}, u32[]{:S(2)}, u32[]{:S(2)}) collective-permute-start(bf16[2,256,256]{1,2,0:T(8,128)(2,1)S(1)} %pad_maximum_fusion.2), channel_id=1, source_target_pairs={{0,16},{8,24},{16,32},{24,40},{32,48},{40,56},{48,64},{56,72},{64,... | collective-permute-start | bytes 786440 | tf_op jit(solution)/shard_map/ppermute | solution.py:21
  15.5 2.2 collective-permute-start.1
  17.7 0.1 copy.68
  17.8 0.1 eq.74
  18.0 0.1 eq.70
  18.1 1.2 reduce-window.18
  19.3 0.2 slice_reduce_fusion.2
  19.6 0.1 fusion.95
  19.7 0.1 reduce_sum.65
  19.8 0.2 slice_reduce_fusion
  20.1 1.1 fusion.52
  21.2 2.8 %add_convert_fusion.1 = bf16[768,2048]{1,0:T(8,128)(2,1)} fusion(f32[768,2048]{1,0:T(8,128)S(1)} %fusion.52, bf16[1,256,2048]{2,1,0:T(8,128)(2,1)S(1)} %copy-done.3, f32[256]{0:T(256)S(1)} %bitcast.201, s32[256]{0:T(256)S(1)} %get-tuple-element.11), kind=kOutput, calls=%fused_computation.9 | convolution fusion | flops 810221568 | bytes 10487808 | tf_op jit(solution)/shard_map/dot_general | solution.py:136
  24.0 7.3 %all-to-all-start = ((bf16[32,24,2048]{2,1,0:T(8,128)(2,1)}), bf16[32,24,2048]{2,1,0:T(8,128)(2,1)}, u32[]{:S(2)}, u32[]{:S(2)}) async-start(bf16[32,24,2048]{2,1,0:T(8,128)(2,1)} %bitcast.189), calls=%async_computation | async-start | bytes 6291456 | tf_op jit(solution)/shard_map/all_to_all | solution.py:139
  31.3 0.1 copy.75
  31.4 0.1 reduce-window.20
  31.4 0.1 reduce.3
  31.6 0.1 convert_reduce_fusion.1
  31.6 0.1 convert_reduce_fusion
  31.8 1.4 and_and_fusion
  33.1 0.1 copy.79
  33.3 2.5 copy.86
  35.8 1.6 fusion.109
  37.4 0.8 copy.77
  38.2 1.0 fusion.110
  39.1 0.1 copy.78
  39.3 10.1 %fusion.112 = (f32[2,8,256]{2,1,0:T(8,128)S(1)}, f32[2,8,256,768]{2,3,1,0:T(8,128)}) fusion(pred[256,768]{0,1:T(8,128)(4,1)S(1)} %copy-done.7, bf16[256,2,8,128]{3,2,1,0:T(8,128)(2,1)} %bitcast.193, bf16[256,2,128]{2,0,1:T(8,128)(2,1)S(1)} %copy.79, bf16[256,2,128]{2,0,1:T(8,128)(2,1)S(1)} %copy.78, bf16[256,2,128]{2,0,1:T(8,128)(2,1)} %copy.77), kind=kOutput, calls=%fused_computation.138 | convolution fusion | flops 819069696 | bytes 14237696 | tf_op jit(solution)/shard_map/sub | solution.py:58
  49.4 6.7 %fusion.36 = bf16[2,128,8,256]{3,1,2,0:T(8,128)(2,1)} fusion(f32[2,8,256,768]{2,3,1,0:T(8,128)} %get-tuple-element.27, f32[2,8,256]{2,1,0:T(8,128)S(1)} %get-tuple-element.26, bf16[256,2,128]{0,2,1:T(8,128)(2,1)S(1)} %bitcast.194, bf16[256,2,128]{0,2,1:T(8,128)(2,1)S(1)} %bitcast.200, bf16[256,2,128]{0,2,1:T(8,128)(2,1)S(1)} %bitcast.199), kind=kOutput, calls=%fused_computation.55 | convolution fusion | flops 813301760 | bytes 14041088 | tf_op jit(solution)/shard_map/kgrs,skd->rkgd/dot_general | solution.py:60
  56.1 17.2 %all-to-all-done = bf16[32,24,2048]{2,1,0:T(8,128)(2,1)} async-done(((bf16[32,24,2048]{2,1,0:T(8,128)(2,1)}), bf16[32,24,2048]{2,1,0:T(8,128)(2,1)}, u32[]{:S(2)}, u32[]{:S(2)}) %all-to-all-start) | async-done | bytes 3145760 | tf_op jit(solution)/shard_map/all_to_all | solution.py:139
  73.3 1.5 all-gather.2.cloned.1.call-done
  74.8 3.8 %fusion.76 = f32[256,2048]{1,0:T(8,128)S(1)} fusion(bf16[1024,2048]{1,0:T(8,128)(2,1)} %all-gather.2.cloned.1.call-done, bf16[256,2048]{0,1:T(8,128)(2,1)} %bitcast.197, s32[]{:T(128)S(6)} %select_n.19), kind=kOutput, calls=%fused_computation.87 | convolution fusion | flops 1073741824 | bytes 6815748 | tf_op jit(solution)/shard_map/dot_general | solution.py:178
  78.6 3.7 %collective-permute-done.2 = bf16[1024,2048]{1,0:T(8,128)(2,1)} collective-permute-done((bf16[1024,2048]{1,0:T(8,128)(2,1)}, bf16[1024,2048]{1,0:T(8,128)(2,1)}, u32[]{:S(2)}, u32[]{:S(2)}) %collective-permute-start.2) | collective-permute-done | bytes 4194336 | tf_op jit(solution)/shard_map/ppermute | solution.py:174
  82.3 3.7 %multiply_reduce_fusion.1 = (f32[256]{0:T(256)S(1)}, f32[256,2048]{1,0:T(8,128)S(1)}) fusion(f32[256,2048]{1,0:T(8,128)S(1)} %fusion.76, bf16[1024,2048]{1,0:T(8,128)(2,1)} %collective-permute-done.2, bf16[256,2048]{0,1:T(8,128)(2,1)S(1)} %bitcast.198, s32[]{:T(128)S(6)} %select_n.21, bf16[1,256,2048]{2,1,0:T(8,128)(2,1)S(1)} %copy-done.5), kind=kOutput, calls=%fused_computation.45 | convolution fusion | flops 1077411584 | bytes 9962500 | tf_op jit(solution)/shard_map/dot_general | solution.py:179
  86.0 2.9 %convolution_convert_fusion.1 = bf16[768,2048]{1,0:T(8,128)(2,1)} fusion(f32[256,2048]{1,0:T(8,128)S(1)} %get-tuple-element.29, f32[2048]{0:T(1024)S(1)} %copy-done.9, f32[256]{0:T(256)S(1)} %fusion.99, s32[256]{0:T(256)S(1)} %get-tuple-element.11, s32[256]{0:T(256)S(1)} %get-tuple-element.12), kind=kOutput, calls=%fused_computation.13 | convolution fusion | flops 810024960 | bytes 5254144 | tf_op jit(solution)/shard_map/dot_general | solution.py:184
  88.9 7.0 %all-to-all-start.1 = ((bf16[32,24,2048]{2,1,0:T(8,128)(2,1)}), bf16[32,24,2048]{2,1,0:T(8,128)(2,1)}, u32[]{:S(2)}, u32[]{:S(2)}) async-start(bf16[32,24,2048]{2,1,0:T(8,128)(2,1)} %bitcast.190), calls=%async_computation.1 | async-start | bytes 6291456 | tf_op jit(solution)/shard_map/all_to_all | solution.py:188
  95.9 0.0 reduce-scatter.3.cloned.1.call-start
  96.0 5.2 %fusion.43 = f32[32,1,24,384]{3,2,0,1:T(8,128)} fusion(bf16[1,384,2048]{2,1,0:T(8,128)(2,1)} %param.24, bf16[32,1,24,2048]{3,2,0,1:T(8,128)(2,1)} %bitcast.9), kind=kOutput, calls=%fused_computation.58 | convolution fusion | flops 1207959552 | bytes 5898240 | tf_op jit(solution)/shard_map/secd,efd->secf/dot_general | solution.py:78
  101.2 36.7 %all-to-all-done.1 = bf16[32,24,2048]{2,1,0:T(8,128)(2,1)} async-done(((bf16[32,24,2048]{2,1,0:T(8,128)(2,1)}), bf16[32,24,2048]{2,1,0:T(8,128)(2,1)}, u32[]{:S(2)}, u32[]{:S(2)}) %all-to-all-start.1) | async-done | bytes 3145760 | tf_op jit(solution)/shard_map/all_to_all | solution.py:188
  137.9 4.2 %fusion.37 = f32[32,1,24,384]{3,2,0,1:T(8,128)S(1)} fusion(bf16[32,24,2048]{2,1,0:T(8,128)(2,1)} %all-to-all-done.1, bf16[1,2048,384]{2,1,0:T(8,128)(2,1)} %param.22), kind=kOutput, calls=%fused_computation.56 | convolution fusion | flops 1207959552 | bytes 5898240 | tf_op jit(solution)/shard_map/secd,edf->secf/dot_general | solution.py:67
  142.2 5.1 %multiply_convert_fusion.3 = (bf16[32,1,24,384]{3,2,0,1:T(8,128)(2,1)}, bf16[32,1,24,384]{3,2,0,1:T(8,128)(2,1)S(1)}, bf16[32,1,24,384]{3,2,0,1:T(8,128)(2,1)S(1)}) fusion(f32[32,1,24,384]{3,2,0,1:T(8,128)S(1)} %fusion.37, f32[32,1,24,384]{3,2,0,1:T(8,128)S(1)} %copy-done.16, bf16[32,24,2048]{2,1,0:T(8,128)(2,1)} %all-to-all-done.1, ...), kind=kOutput, calls=%fused_computation.62 | convolution fusion | flops 1212678144 | bytes 8847360 | tf_op jit(solution)/shard_map/secd,edf->secf/dot_general | solution.py:68
  147.3 4.6 %fusion.32 = f32[32,24,2048]{2,1,0:T(8,128)} fusion(bf16[1,2048,384]{2,1,0:T(8,128)(2,1)S(1)} %copy-done.4, bf16[32,1,24,384]{3,2,0,1:T(8,128)(2,1)S(1)} %get-tuple-element.16), kind=kOutput, calls=%fused_computation.51 | convolution fusion | flops 1207959552 | bytes 8454144 | tf_op jit(solution)/shard_map/secf,edf->secd/dot_general | solution.py:88
  151.9 3.7 %fusion.14 = bf16[1,2048,384]{2,1,0:T(8,128)(2,1)S(1)} fusion(bf16[32,24,2048]{2,1,0:T(8,128)(2,1)} %all-to-all-done.1, bf16[32,1,24,384]{3,2,0,1:T(8,128)(2,1)S(1)} %get-tuple-element.16), kind=kOutput, calls=%fused_computation.32 | convolution fusion | flops 1208745984 | bytes 5308416 | tf_op jit(solution)/shard_map/secd,secf->edf/dot_general | solution.py:84
  155.6 3.7 %fusion.15 = bf16[1,2048,384]{2,1,0:T(8,128)(2,1)S(1)} fusion(bf16[32,24,2048]{2,1,0:T(8,128)(2,1)} %all-to-all-done.1, bf16[32,1,24,384]{3,2,0,1:T(8,128)(2,1)S(1)} %get-tuple-element.17), kind=kOutput, calls=%fused_computation.33 | convolution fusion | flops 1208745984 | bytes 5308416 | tf_op jit(solution)/shard_map/secd,secf->edf/dot_general | solution.py:87
  159.3 2.0 pad_maximum_fusion.1
  161.4 0.0 reduce-scatter.3.cloned.1.call-update
  161.4 4.8 %add_convert_fusion = bf16[32,24,2048]{2,1,0:T(8,128)(2,1)S(1)} fusion(f32[32,24,2048]{2,1,0:T(8,128)} %fusion.32, bf16[1,2048,384]{2,1,0:T(8,128)(2,1)S(1)} %copy-done, bf16[32,1,24,384]{3,2,0,1:T(8,128)(2,1)S(1)} %get-tuple-element.17), kind=kOutput, calls=%fused_computation.6 | convolution fusion | flops 1211105280 | bytes 11599872 | tf_op jit(solution)/shard_map/secf,edf->secd/dot_general | solution.py:91
  166.2 2.0 convolution_convert_fusion
  168.2 3.8 %pad_maximum_fusion = bf16[32,48,2048]{2,1,0:T(8,128)(2,1)} fusion(bf16[32,24,2048]{2,1,0:T(8,128)(2,1)S(1)} %add_convert_fusion, bf16[32,24,2048]{2,1,0:T(8,128)(2,1)S(1)} %convolution_convert_fusion), kind=kLoop, calls=%fused_computation.5 | loop fusion | flops 12582912 | bytes 12582912 | tf_op jit(solution)/shard_map/concatenate | solution.py:196
  172.0 5.0 %all-to-all-start.2 = ((bf16[32,48,2048]{2,1,0:T(8,128)(2,1)}), bf16[32,48,2048]{2,1,0:T(8,128)(2,1)}, u32[]{:S(2)}, u32[]{:S(2)}) async-start(bf16[32,48,2048]{2,1,0:T(8,128)(2,1)} %pad_maximum_fusion), calls=%async_computation.2 | async-start | bytes 12582912 | tf_op jit(solution)/shard_map/all_to_all | solution.py:195
  177.0 0.0 reduce-scatter.5.cloned.1.call-start
  177.1 4.5 %fusion.16 = bf16[1,384,2048]{2,1,0:T(8,128)(2,1)} fusion(bf16[32,1,24,2048]{3,2,0,1:T(8,128)(2,1)} %bitcast.9, bf16[32,1,24,384]{3,2,0,1:T(8,128)(2,1)S(1)} %copy-done.15), kind=kOutput, calls=%fused_computation.34 | convolution fusion | flops 1208745984 | bytes 5308416 | tf_op jit(solution)/shard_map/secf,secd->efd/dot_general | solution.py:77
  181.6 0.0 reduce-scatter.5.cloned.1.call-update
  181.7 73.3 %all-to-all-done.2 = bf16[32,48,2048]{2,1,0:T(8,128)(2,1)} async-done(((bf16[32,48,2048]{2,1,0:T(8,128)(2,1)}), bf16[32,48,2048]{2,1,0:T(8,128)(2,1)}, u32[]{:S(2)}, u32[]{:S(2)}) %all-to-all-start.2) | async-done | bytes 6291488 | tf_op jit(solution)/shard_map/all_to_all | solution.py:195
  254.9 3.6 %fusion.107 = (bf16[32,24,2048]{2,1,0:T(8,128)(2,1)S(1)}, bf16[32,24,2048]{2,1,0:T(8,128)(2,1)S(1)}) fusion(bf16[32,48,2048]{2,1,0:T(8,128)(2,1)} %all-to-all-done.2), kind=kLoop, calls=%fused_computation.133 | loop fusion | bytes 12582912 | tf_op jit(solution)/shard_map/slice | solution.py:205
  258.5 1.1 multiply_reduce_fusion
  259.7 1.0 convolution_multiply_fusion.2
  260.7 2.0 fusion.23
  262.7 1.5 fusion.50
  264.2 1.8 fusion.108
  (49 shorter events, 0.2 us)
Async XLA Ops:
  7.2 135.0 %copy-start = (bf16[1,2048,384]{2,1,0:T(8,128)(2,1)S(1)}, bf16[1,2048,384]{2,1,0:T(8,128)(2,1)}, u32[]{:S(2)}) copy-start(bf16[1,2048,384]{2,1,0:T(8,128)(2,1)} %param.23) | copy-start | bytes 4718596
  7.2 10.5 %copy-start.10 = (s32[1,256,2]{1,2,0:T(2,128)S(1)}, s32[1,256,2]{1,2,0:T(2,128)}, u32[]{:S(2)}) copy-start(s32[1,256,2]{1,2,0:T(2,128)} %param.20) | copy-start | bytes 6148
  7.2 67.6 %all-gather.2.cloned.1.call-start = ((), (), s32[]{:S(2)}) async-start(), calls=%async_computation.5 | async-start | bytes 4718592 | tf_op jit(solution)/shard_map/all_gather | solution.py:146
  7.2 12.8 %copy-start.11 = (f32[1,256,2]{1,2,0:T(2,128)S(1)}, f32[1,256,2]{1,2,0:T(2,128)}, u32[]{:S(2)}) copy-start(f32[1,256,2]{1,2,0:T(2,128)} %param.21) | copy-start | bytes 6148
  7.3 12.8 %copy-start.3 = (bf16[1,256,2048]{2,1,0:T(8,128)(2,1)S(1)}, bf16[1,256,2048]{2,1,0:T(8,128)(2,1)}, u32[]{:S(2)}) copy-start(bf16[1,256,2048]{2,1,0:T(8,128)(2,1)} %param.25) | copy-start | bytes 3145732
  11.4 24.4 %collective-permute-start = (bf16[2,256,256]{1,2,0:T(8,128)(2,1)S(1)}, bf16[2,256,256]{1,2,0:T(8,128)(2,1)}, u32[]{:S(2)}, u32[]{:S(2)}) collective-permute-start(bf16[2,256,256]{1,2,0:T(8,128)(2,1)S(1)} %pad_maximum_fusion.2), channel_id=1, source_target_pairs={{0,16},{8,24},{16,32},{24,40},{32,48},{40,56},{48,64},{56,72},{64,... | collective-permute-start | bytes 786440 | tf_op jit(solution)/shard_map/ppermute | solution.py:21
  15.5 22.7 %collective-permute-start.1 = (bf16[2,256,256]{1,2,0:T(8,128)(2,1)S(1)}, bf16[2,256,256]{1,2,0:T(8,128)(2,1)}, u32[]{:S(2)}, u32[]{:S(2)}) collective-permute-start(bf16[2,256,256]{1,2,0:T(8,128)(2,1)S(1)} %pad_maximum_fusion.2), channel_id=1, source_target_pairs={{0,8},{8,16},{16,24},{24,32},{32,40},{40,48},{48,56},{56,64},{64,7... | collective-permute-start | bytes 786440 | tf_op jit(solution)/shard_map/ppermute | solution.py:21
  24.0 7.3 %copy-start.12 = (s32[1,32]{1,0:T(1,128)S(1)}, s32[1,32]{1,0:T(1,128)}, u32[]{:S(2)}) copy-start(s32[1,32]{1,0:T(1,128)} %param.16) | copy-start | bytes 388
  24.0 49.3 %all-to-all-start = ((bf16[32,24,2048]{2,1,0:T(8,128)(2,1)}), bf16[32,24,2048]{2,1,0:T(8,128)(2,1)}, u32[]{:S(2)}, u32[]{:S(2)}) async-start(bf16[32,24,2048]{2,1,0:T(8,128)(2,1)} %bitcast.189), calls=%async_computation | async-start | bytes 6291456 | tf_op jit(solution)/shard_map/all_to_all | solution.py:139
  33.2 6.0 %copy-start.7 = (pred[256,768]{0,1:T(8,128)(4,1)S(1)}, pred[256,768]{0,1:T(8,128)(4,1)}, u32[]{:S(2)}) copy-start(pred[256,768]{0,1:T(8,128)(4,1)} %and_and_fusion) | copy-start | bytes 589828
  39.3 10.1 %copy-start.8 = (bf16[1,256,256]{1,2,0:T(8,128)(2,1)S(1)}, bf16[1,256,256]{1,2,0:T(8,128)(2,1)}, u32[]{:S(2)}) copy-start(bf16[1,256,256]{1,2,0:T(8,128)(2,1)} %get-tuple-element.20) | copy-start | bytes 393220
  74.8 7.5 %collective-permute-start.2 = (bf16[1024,2048]{1,0:T(8,128)(2,1)}, bf16[1024,2048]{1,0:T(8,128)(2,1)}, u32[]{:S(2)}, u32[]{:S(2)}) collective-permute-start(bf16[1024,2048]{1,0:T(8,128)(2,1)} %all-gather.2.cloned.1.call-done), channel_id=1, source_target_pairs={{0,8},{8,0},{16,24},{24,16},{32,40},{40,32},{48,56},{56,48},{64,72... | collective-permute-start | bytes 12582920 | tf_op jit(solution)/shard_map/ppermute | solution.py:174
  74.8 7.5 %copy-start.5 = (bf16[1,256,2048]{2,1,0:T(8,128)(2,1)S(1)}, bf16[1,256,2048]{2,1,0:T(8,128)(2,1)}, u32[]{:S(2)}) copy-start(bf16[1,256,2048]{2,1,0:T(8,128)(2,1)} %param.17) | copy-start | bytes 3145732
  74.8 7.5 %copy-start.6 = (bf16[2,128,8,256]{3,1,2,0:T(8,128)(2,1)S(1)}, bf16[2,128,8,256]{3,1,2,0:T(8,128)(2,1)}, u32[]{:S(2)}) copy-start(bf16[2,128,8,256]{3,1,2,0:T(8,128)(2,1)} %fusion.36) | copy-start | bytes 3145732
  78.5 7.5 %copy-start.9 = (f32[2048]{0:T(1024)S(1)}, f32[2048]{0:T(1024)}, u32[]{:S(2)}) copy-start(f32[2048]{0:T(1024)} %param.19) | copy-start | bytes 24580
  86.0 2.9 %copy-start.1 = (f32[256,2048]{1,0:T(8,128)}, f32[256,2048]{1,0:T(8,128)S(1)}, u32[]{:S(2)}) copy-start(f32[256,2048]{1,0:T(8,128)S(1)} %get-tuple-element.29) | copy-start | bytes 6291460
  88.9 49.0 %all-to-all-start.1 = ((bf16[32,24,2048]{2,1,0:T(8,128)(2,1)}), bf16[32,24,2048]{2,1,0:T(8,128)(2,1)}, u32[]{:S(2)}, u32[]{:S(2)}) async-start(bf16[32,24,2048]{2,1,0:T(8,128)(2,1)} %bitcast.190), calls=%async_computation.1 | async-start | bytes 6291456 | tf_op jit(solution)/shard_map/all_to_all | solution.py:188
  95.9 168.3 %reduce-scatter.3.cloned.1.call-start = ((), (), s32[]{:S(2)}) async-start(), calls=%async_computation.6 | async-start | bytes 3538944 | tf_op jit(solution)/shard_map/reduce_scatter | solution.py:228
  137.9 4.3 %copy-start.16 = (f32[32,1,24,384]{3,2,0,1:T(8,128)S(1)}, f32[32,1,24,384]{3,2,0,1:T(8,128)}, u32[]{:S(2)}) copy-start(f32[32,1,24,384]{3,2,0,1:T(8,128)} %fusion.43) | copy-start | bytes 3538948
  142.2 5.1 %copy-start.4 = (bf16[1,2048,384]{2,1,0:T(8,128)(2,1)S(1)}, bf16[1,2048,384]{2,1,0:T(8,128)(2,1)}, u32[]{:S(2)}) copy-start(bf16[1,2048,384]{2,1,0:T(8,128)(2,1)} %param.22) | copy-start | bytes 4718596
  161.4 4.8 %copy-start.13 = (bf16[1,384,2048]{2,1,0:T(8,128)(2,1)S(1)}, bf16[1,384,2048]{2,1,0:T(8,128)(2,1)}, u32[]{:S(2)}) copy-start(bf16[1,384,2048]{2,1,0:T(8,128)(2,1)} %param.24) | copy-start | bytes 4718596
  161.4 4.8 %copy-start.14 = (bf16[32,1,24,384]{3,2,0,1:T(8,128)(2,1)S(1)}, bf16[32,1,24,384]{3,2,0,1:T(8,128)(2,1)}, u32[]{:S(2)}) copy-start(bf16[32,1,24,384]{3,2,0,1:T(8,128)(2,1)} %get-tuple-element.15) | copy-start | bytes 1769476
  172.0 5.1 %copy-start.15 = (bf16[32,1,24,384]{3,2,0,1:T(8,128)(2,1)S(1)}, bf16[32,1,24,384]{3,2,0,1:T(8,128)(2,1)}, u32[]{:S(2)}) copy-start(bf16[32,1,24,384]{3,2,0,1:T(8,128)(2,1)} %get-tuple-element.15) | copy-start | bytes 1769476
  172.0 82.9 %all-to-all-start.2 = ((bf16[32,48,2048]{2,1,0:T(8,128)(2,1)}), bf16[32,48,2048]{2,1,0:T(8,128)(2,1)}, u32[]{:S(2)}, u32[]{:S(2)}) async-start(bf16[32,48,2048]{2,1,0:T(8,128)(2,1)} %pad_maximum_fusion), calls=%async_computation.2 | async-start | bytes 12582912 | tf_op jit(solution)/shard_map/all_to_all | solution.py:195
  177.0 89.0 %reduce-scatter.5.cloned.1.call-start = ((), (), s32[]{:S(2)}) async-start(), calls=%async_computation.7 | async-start | bytes 1769472 | tf_op jit(solution)/shard_map/reduce_scatter | solution.py:234
  254.9 3.6 %copy-start.2 = (f32[256,2048]{1,0:T(8,128)S(1)}, f32[256,2048]{1,0:T(8,128)}, u32[]{:S(2)}) copy-start(f32[256,2048]{1,0:T(8,128)} %copy-done.1) | copy-start | bytes 6291460
Sparse Core Ops, SparseCore 0:
  10.3 64.4 all-gather.1
  161.5 40.6 reduce-scatter.2
  205.3 40.0 reduce-scatter.4

commit v5 on v1

--- a/solution.py
+++ b/solution.py
@@ -171,12 +171,16 @@
         key_places,
     )
     grads_arrived, mine, attended = lax.optimization_barrier((grads_arrived, mine, attended))
-    other = lax.ppermute(mine, "seq", [(i, i ^ 1) for i in range(seq_count)])
+    piece = half // 2
+    pairs = [(i, i ^ 1) for i in range(seq_count)]
+    other_first = lax.ppermute(mine[:piece], "seq", pairs)
+    other_second = lax.ppermute(mine[piece:], "seq", pairs)
     attended_mine = lax.dynamic_slice_in_dim(attended, core * half, half, axis=1)
     attended_other = lax.dynamic_slice_in_dim(attended, (1 - core) * half, half, axis=1)
     projected = (
         jnp.dot(attended_mine, mine, preferred_element_type=jnp.float32)
-        + jnp.dot(attended_other, other, preferred_element_type=jnp.float32)
+        + jnp.dot(attended_other[:, :piece], other_first, preferred_element_type=jnp.float32)
+        + jnp.dot(attended_other[:, piece:], other_second, preferred_element_type=jnp.float32)
     ).astype(jnp.bfloat16)
     stream = residual[0].astype(jnp.float32) + projected.astype(jnp.float32)
     normalized = normed(stream, norm_gain).astype(jnp.bfloat16)

time: 258 us -> 261 us (1.012)
  local copies, waits for them, and re-layouts: 11.1 us -> 15.9 us
  waiting for transfers between devices: 92.6 us -> 89.8 us
    slice x1 -> x2, local copies, waits for them, and re-layouts: 0.22 us -> 4.96 us  [the longest x1 4.74 us: body(): other_second = lax.ppermute(mine[piece:], 'seq', pairs)]
    ppermute x1 -> x2, waiting for transfers between devices: 3.94 us -> 1.16 us  [the longest x1 0.64 us: body(): other_second = lax.ppermute(mine[piece:], 'seq', pairs)]
  transfers between devices with their start and end apart: 9 -> 10, of which waited for: 5 -> 6; matrix products, arithmetic and copies ran while one was open for 22% -> 22% of each run, Pallas kernels for 0% -> 0%
where the time goes in v5:
time: 261 us
  waiting for transfers between devices  89.8 us (34%)
  matrix products  64.1 us (25%)
  blocking collectives  46.7 us (18%)
  starting transfers between devices  23.3 us (9%)
  local copies, waits for them, and re-layouts  15.9 us (6%)
  between operations  14.3 us (5%)
  other arithmetic  6.66 us (3%)
    all_to_all x1, blocking collectives, body(): lax.all_to_all(outgoing, 'seq', split_axis=0, concat_axis=0, tiled=True)  46.7 us
    all_to_all x1, waiting for transfers between devices, body(): lax.all_to_all(expert_out.reshape(sent_shape), 'seq', split_axis=0, conca...  34.6 us
    all_to_all x1, waiting for transfers between devices, body(): lax.all_to_all(grad_inputs.reshape(sent_shape), 'seq', split_axis=0, conc...  31.7 us
    all_to_all x1, waiting for transfers between devices, body(): lax.all_to_all(grads_outgoing, 'seq', split_axis=0, concat_axis=0, tiled=...  20.8 us
    sub x1, matrix products, attend_block(): raised = jnp.exp(scores - row_max)  10 us
    all_to_all x1, starting transfers between devices, body(): lax.all_to_all(grads_outgoing, 'seq', split_axis=0, concat_axis=0, tiled=...  7.3 us
    ppermute x2, starting transfers between devices, from_behind(): return lax.ppermute(shard, axis, pairs)  6.25 us
    dot_general x1, matrix products, attend_block(): jnp.einsum('kgrs,skd->rkgd', probs, values_all.reshape(-1, KV, HD), prefe...  5.69 us
  transfers between devices with their start and end apart: 10, of which 6 were waited for; matrix products, arithmetic and copies ran while one was open for 22% of the time, Pallas kernels for 0%

profile of v5, /device:TPU:32, one launch (start us, length us, event | category | flops | bytes accessed | tf_op | source)
XLA Modules:
  0.0 260.8 jit_solution(4949597069520054597)
XLA Ops:
  7.3 2.0 constant_dynamic-slice_fusion
  9.3 1.0 copy.72
  10.3 1.0 copy.73
  11.4 4.1 %collective-permute-start = (bf16[2,256,256]{1,2,0:T(8,128)(2,1)S(1)}, bf16[2,256,256]{1,2,0:T(8,128)(2,1)}, u32[]{:S(2)}, u32[]{:S(2)}) collective-permute-start(bf16[2,256,256]{1,2,0:T(8,128)(2,1)S(1)} %pad_maximum_fusion.1), channel_id=1, source_target_pairs={{0,16},{8,24},{16,32},{24,40},{32,48},{40,56},{48,64},{56,72},{64,... | collective-permute-start | bytes 786440 | tf_op jit(solution)/shard_map/ppermute | solution.py:21
  15.5 2.2 collective-permute-start.1
  17.6 0.1 copy.68
  17.8 0.1 eq.74
  17.9 0.1 eq.70
  18.1 1.2 reduce-window.18
  19.3 0.2 slice_reduce_fusion.2
  19.5 0.1 fusion.110
  19.6 0.1 reduce_sum.65
  19.8 0.2 slice_reduce_fusion
  20.1 1.1 fusion.66
  21.1 2.8 %add_convert_fusion.1 = bf16[768,2048]{1,0:T(8,128)(2,1)} fusion(f32[768,2048]{1,0:T(8,128)S(1)} %fusion.66, bf16[1,256,2048]{2,1,0:T(8,128)(2,1)S(1)} %copy-done.7, f32[256]{0:T(256)S(1)} %bitcast.237, s32[256]{0:T(256)S(1)} %get-tuple-element.27), kind=kOutput, calls=%fused_computation.8 | convolution fusion | flops 810221568 | bytes 10487808 | tf_op jit(solution)/shard_map/dot_general | solution.py:136
  23.9 7.3 %all-to-all-start = ((bf16[32,24,2048]{2,1,0:T(8,128)(2,1)}), bf16[32,24,2048]{2,1,0:T(8,128)(2,1)}, u32[]{:S(2)}, u32[]{:S(2)}) async-start(bf16[32,24,2048]{2,1,0:T(8,128)(2,1)} %bitcast.220), calls=%async_computation | async-start | bytes 6291456 | tf_op jit(solution)/shard_map/all_to_all | solution.py:139
  31.2 0.0 reduce-scatter.3.cloned.1.call-start
  31.3 0.1 copy.75
  31.4 0.1 reduce-window.20
  31.4 0.1 reduce.3
  31.6 0.1 convert_reduce_fusion.1
  31.7 0.1 convert_reduce_fusion
  31.8 1.4 and_and_fusion
  33.1 0.1 copy.79
  33.3 1.2 copy.86
  34.5 1.0 fusion.125
  35.5 0.1 copy.77
  35.6 1.0 fusion.126
  36.6 0.1 copy.78
  36.7 10.0 %fusion.128 = (f32[2,8,256]{2,1,0:T(8,128)S(1)}, f32[2,8,256,768]{2,3,1,0:T(8,128)}) fusion(pred[256,768]{0,1:T(8,128)(4,1)S(1)} %copy-done.17, bf16[256,2,8,128]{3,2,1,0:T(8,128)(2,1)} %bitcast.228, bf16[256,2,128]{2,0,1:T(8,128)(2,1)S(1)} %copy.79, bf16[256,2,128]{2,0,1:T(8,128)(2,1)S(1)} %copy.78, bf16[256,2,128]{2,0,1:T(8,128)(2,1)S(1)} %copy.77), kind=kOutput, calls=%fused_computation.146 | convolution fusion | flops 819069696 | bytes 14237696 | tf_op jit(solution)/shard_map/sub | solution.py:58
  46.8 5.7 %fusion.50 = bf16[2,128,8,256]{3,1,2,0:T(8,128)(2,1)S(1)} fusion(f32[2,8,256,768]{2,3,1,0:T(8,128)} %get-tuple-element.42, f32[2,8,256]{2,1,0:T(8,128)S(1)} %get-tuple-element.41, bf16[256,2,128]{0,2,1:T(8,128)(2,1)S(1)} %bitcast.229, bf16[256,2,128]{0,2,1:T(8,128)(2,1)S(1)} %bitcast.236, bf16[256,2,128]{0,2,1:T(8,128)(2,1)S(1)} %bitcast.235), kind=kOutput, calls=%fused_computation.61 | convolution fusion | flops 813301760 | bytes 14041088 | tf_op jit(solution)/shard_map/kgrs,skd->rkgd/dot_general | solution.py:60
  52.5 20.8 %all-to-all-done = bf16[32,24,2048]{2,1,0:T(8,128)(2,1)} async-done(((bf16[32,24,2048]{2,1,0:T(8,128)(2,1)}), bf16[32,24,2048]{2,1,0:T(8,128)(2,1)}, u32[]{:S(2)}, u32[]{:S(2)}) %all-to-all-start) | async-done | bytes 3145760 | tf_op jit(solution)/shard_map/all_to_all | solution.py:139
  73.2 1.6 all-gather.2.cloned.1.call-done
  74.8 4.7 %fusion.123 = (bf16[512,2048]{1,0:T(8,128)(2,1)}, bf16[512,2048]{1,0:T(8,128)(2,1)}) fusion(bf16[1024,2048]{1,0:T(8,128)(2,1)} %all-gather.2.cloned.1.call-done), kind=kLoop, calls=%fused_computation.141 | loop fusion | bytes 8388608 | tf_op jit(solution)/shard_map/slice | solution.py:177
  79.5 0.5 collective-permute-start.3
  80.0 3.5 %fusion.89 = f32[256,2048]{1,0:T(8,128)S(1)} fusion(bf16[1024,2048]{1,0:T(8,128)(2,1)} %all-gather.2.cloned.1.call-done, bf16[256,2048]{0,1:T(8,128)(2,1)S(1)} %bitcast.232, s32[]{:T(128)S(6)} %select_n.19), kind=kOutput, calls=%fused_computation.92 | convolution fusion | flops 1073741824 | bytes 6815748 | tf_op jit(solution)/shard_map/dot_general | solution.py:181
  83.5 0.5 collective-permute-done.2
  84.0 2.3 convolution_add_fusion.1
  86.4 0.6 collective-permute-done.3
  87.0 2.6 multiply_reduce_fusion.1
  89.6 1.1 convolution_convert_fusion.1
  90.8 0.2 copy-done.2
  90.9 46.7 %all_to_all.20 = bf16[32,24,2048]{2,1,0:T(8,128)(2,1)S(1)} all-to-all(bf16[32,24,2048]{2,1,0:T(8,128)(2,1)S(1)} %bitcast.222), channel_id=1, replica_groups=mesh['seq'=32,'dp'=8] {'seq'}, dimensions={0} | all-to-all | bytes 6291456 | tf_op jit(solution)/shard_map/all_to_all | solution.py:192
  137.6 1.8 fusion.51
  139.5 1.9 multiply_convert_fusion.3
  141.4 3.5 %fusion.14 = bf16[32,1,24,2048]{3,2,0,1:T(8,128)(2,1)} fusion(bf16[1,384,2048]{2,1,0:T(8,128)(2,1)S(1)} %copy-done, bf16[32,1,24,384]{3,2,0,1:T(8,128)(2,1)S(1)} %get-tuple-element.26), kind=kOutput, calls=%fused_computation.29 | convolution fusion | flops 1209532416 | bytes 5308416 | tf_op jit(solution)/shard_map/secf,efd->secd/dot_general | solution.py:70
  144.9 4.0 %multiply_convert_fusion.1 = (bf16[32,1,24,384]{3,2,0,1:T(8,128)(2,1)S(1)}, bf16[32,1,24,384]{3,2,0,1:T(8,128)(2,1)S(1)}) fusion(f32[32,1,24,384]{3,2,0,1:T(8,128)S(1)} %fusion.51, f32[32,1,24,384]{3,2,0,1:T(8,128)S(1)} %get-tuple-element.21, bf16[1,384,2048]{2,1,0:T(8,128)(2,1)S(1)} %copy-done, bf16[32,1,24,2048]{3,2,0,1:T(8,128)(2,1)} %bitcast.9), kind=kOutput, calls=%fused_computation.66 | convolution fusion | flops 1211793408 | bytes 8257536 | tf_op jit(solution)/shard_map/secd,efd->secf/dot_general | solution.py:78
  148.9 1.9 fusion.25
  150.8 1.9 fusion.28
  152.7 2.0 pad_maximum_fusion
  154.7 4.3 %all-to-all-start.2 = ((bf16[32,24,2048]{2,1,0:T(8,128)(2,1)}), bf16[32,24,2048]{2,1,0:T(8,128)(2,1)S(1)}, u32[]{:S(2)}, u32[]{:S(2)}) async-start(bf16[32,24,2048]{2,1,0:T(8,128)(2,1)} %bitcast.223), calls=%async_computation.2 | async-start | bytes 6291456 | tf_op jit(solution)/shard_map/all_to_all | solution.py:199
  159.1 3.6 %fusion.46 = f32[32,24,2048]{2,1,0:T(8,128)S(1)} fusion(bf16[1,2048,384]{2,1,0:T(8,128)(2,1)} %param.22, bf16[32,1,24,384]{3,2,0,1:T(8,128)(2,1)} %copy-done.16), kind=kOutput, calls=%fused_computation.57 | convolution fusion | flops 1207959552 | bytes 8454144 | tf_op jit(solution)/shard_map/secf,edf->secd/dot_general | solution.py:88
  162.7 3.5 %fusion.15 = bf16[32,1,24,2048]{3,2,0,1:T(8,128)(2,1)} fusion(f32[32,24,2048]{2,1,0:T(8,128)S(1)} %fusion.46, bf16[1,2048,384]{2,1,0:T(8,128)(2,1)S(1)} %copy-done.11, bf16[32,1,24,384]{3,2,0,1:T(8,128)(2,1)S(1)} %copy-done.15), kind=kOutput, calls=%fused_computation.30 | convolution fusion | flops 1211105280 | bytes 11599872 | tf_op jit(solution)/shard_map/secf,edf->secd/dot_general | solution.py:91
  166.2 34.6 %all-to-all-done.2 = bf16[32,24,2048]{2,1,0:T(8,128)(2,1)S(1)} async-done(((bf16[32,24,2048]{2,1,0:T(8,128)(2,1)}), bf16[32,24,2048]{2,1,0:T(8,128)(2,1)S(1)}, u32[]{:S(2)}, u32[]{:S(2)}) %all-to-all-start.2) | async-done | bytes 3145760 | tf_op jit(solution)/shard_map/all_to_all | solution.py:199
  200.8 4.8 %all-to-all-start.3 = ((bf16[32,24,2048]{2,1,0:T(8,128)(2,1)}), bf16[32,24,2048]{2,1,0:T(8,128)(2,1)}, u32[]{:S(2)}, u32[]{:S(2)}) async-start(bf16[32,24,2048]{2,1,0:T(8,128)(2,1)} %bitcast.221), calls=%async_computation.3 | async-start | bytes 6291456 | tf_op jit(solution)/shard_map/all_to_all | solution.py:206
  205.7 0.0 reduce-scatter.5.cloned.1.call-start
  205.7 4.7 %fusion.31 = bf16[1,384,2048]{2,1,0:T(8,128)(2,1)} fusion(bf16[32,1,24,2048]{3,2,0,1:T(8,128)(2,1)} %bitcast.9, bf16[32,1,24,384]{3,2,0,1:T(8,128)(2,1)} %copy-done.22), kind=kOutput, calls=%fused_computation.41 | convolution fusion | flops 1208745984 | bytes 5308416 | tf_op jit(solution)/shard_map/secf,secd->efd/dot_general | solution.py:77
  210.4 3.1 %convolution_multiply_fusion.2 = f32[256,2048]{1,0:T(8,128)S(1)} fusion(bf16[768,2048]{1,0:T(8,128)(2,1)} %bitcast.218, f32[256]{0:T(256)S(1)} %bitcast.240, s32[256]{0:T(256)S(1)} %get-tuple-element.28), kind=kOutput, calls=%fused_computation.34 | convolution fusion | flops 806027264 | bytes 5244928 | tf_op jit(solution)/shard_map/dot_general | solution.py:212
  213.5 0.4 copy-done.6
  213.9 2.1 fusion.37
  216.0 31.7 %all-to-all-done.3 = bf16[32,24,2048]{2,1,0:T(8,128)(2,1)} async-done(((bf16[32,24,2048]{2,1,0:T(8,128)(2,1)}), bf16[32,24,2048]{2,1,0:T(8,128)(2,1)}, u32[]{:S(2)}, u32[]{:S(2)}) %all-to-all-start.3) | async-done | bytes 3145760 | tf_op jit(solution)/shard_map/all_to_all | solution.py:206
  247.7 3.2 %multiply_reduce_fusion = (f32[256]{0:T(256)S(1)}, f32[256,2048]{1,0:T(8,128)S(1)}) fusion(f32[256,2048]{1,0:T(8,128)S(1)} %copy-done.3, f32[2048]{0:T(1024)S(1)} %copy-done.18, bf16[768,2048]{1,0:T(8,128)(2,1)} %bitcast.59, s32[256]{0:T(256)S(1)} %get-tuple-element.27, s32[256]{0:T(256)S(1)} %get-tuple-element.28), kind=kOutput, calls=%fused_computation.49 | convolution fusion | flops 808451840 | bytes 7351296 | tf_op jit(solution)/shard_map/dot_general | solution.py:221
  250.9 1.5 fusion.64
  252.4 1.8 fusion.124
  (64 shorter events, 0.3 us)
Async XLA Ops:
  7.2 134.2 %copy-start = (bf16[1,384,2048]{2,1,0:T(8,128)(2,1)S(1)}, bf16[1,384,2048]{2,1,0:T(8,128)(2,1)}, u32[]{:S(2)}) copy-start(bf16[1,384,2048]{2,1,0:T(8,128)(2,1)} %param.24) | copy-start | bytes 4718596
  7.2 10.5 %copy-start.19 = (s32[1,256,2]{1,2,0:T(2,128)S(1)}, s32[1,256,2]{1,2,0:T(2,128)}, u32[]{:S(2)}) copy-start(s32[1,256,2]{1,2,0:T(2,128)} %param.20) | copy-start | bytes 6148
  7.2 67.6 %all-gather.2.cloned.1.call-start = ((), (), s32[]{:S(2)}) async-start(), calls=%async_computation.6 | async-start | bytes 4718592 | tf_op jit(solution)/shard_map/all_gather | solution.py:146
  7.2 12.8 %copy-start.20 = (f32[1,256,2]{1,2,0:T(2,128)S(1)}, f32[1,256,2]{1,2,0:T(2,128)}, u32[]{:S(2)}) copy-start(f32[1,256,2]{1,2,0:T(2,128)} %param.21) | copy-start | bytes 6148
  7.3 12.8 %copy-start.7 = (bf16[1,256,2048]{2,1,0:T(8,128)(2,1)S(1)}, bf16[1,256,2048]{2,1,0:T(8,128)(2,1)}, u32[]{:S(2)}) copy-start(bf16[1,256,2048]{2,1,0:T(8,128)(2,1)} %param.25) | copy-start | bytes 3145732
  11.4 23.1 %collective-permute-start = (bf16[2,256,256]{1,2,0:T(8,128)(2,1)S(1)}, bf16[2,256,256]{1,2,0:T(8,128)(2,1)}, u32[]{:S(2)}, u32[]{:S(2)}) collective-permute-start(bf16[2,256,256]{1,2,0:T(8,128)(2,1)S(1)} %pad_maximum_fusion.1), channel_id=1, source_target_pairs={{0,16},{8,24},{16,32},{24,40},{32,48},{40,56},{48,64},{56,72},{64,... | collective-permute-start | bytes 786440 | tf_op jit(solution)/shard_map/ppermute | solution.py:21
  15.5 20.1 %collective-permute-start.1 = (bf16[2,256,256]{1,2,0:T(8,128)(2,1)S(1)}, bf16[2,256,256]{1,2,0:T(8,128)(2,1)}, u32[]{:S(2)}, u32[]{:S(2)}) collective-permute-start(bf16[2,256,256]{1,2,0:T(8,128)(2,1)S(1)} %pad_maximum_fusion.1), channel_id=1, source_target_pairs={{0,8},{8,16},{16,24},{24,32},{32,40},{40,48},{48,56},{56,64},{64,7... | collective-permute-start | bytes 786440 | tf_op jit(solution)/shard_map/ppermute | solution.py:21
  23.9 7.4 %copy-start.21 = (s32[1,32]{1,0:T(1,128)S(1)}, s32[1,32]{1,0:T(1,128)}, u32[]{:S(2)}) copy-start(s32[1,32]{1,0:T(1,128)} %param.16) | copy-start | bytes 388
  23.9 9.4 %copy-start.12 = (bf16[1,256,2048]{2,1,0:T(8,128)(2,1)S(1)}, bf16[1,256,2048]{2,1,0:T(8,128)(2,1)}, u32[]{:S(2)}) copy-start(bf16[1,256,2048]{2,1,0:T(8,128)(2,1)} %param.13) | copy-start | bytes 3145732
  23.9 49.3 %all-to-all-start = ((bf16[32,24,2048]{2,1,0:T(8,128)(2,1)}), bf16[32,24,2048]{2,1,0:T(8,128)(2,1)}, u32[]{:S(2)}, u32[]{:S(2)}) async-start(bf16[32,24,2048]{2,1,0:T(8,128)(2,1)} %bitcast.220), calls=%async_computation | async-start | bytes 6291456 | tf_op jit(solution)/shard_map/all_to_all | solution.py:139
  31.2 221.2 %reduce-scatter.3.cloned.1.call-start = ((), (), s32[]{:S(2)}) async-start(), calls=%async_computation.7 | async-start | bytes 3538944 | tf_op jit(solution)/shard_map/reduce_scatter | solution.py:231
  33.3 3.5 %copy-start.17 = (pred[256,768]{0,1:T(8,128)(4,1)S(1)}, pred[256,768]{0,1:T(8,128)(4,1)}, u32[]{:S(2)}) copy-start(pred[256,768]{0,1:T(8,128)(4,1)} %and_and_fusion) | copy-start | bytes 589828
  79.5 4.5 %collective-permute-start.2 = (bf16[512,2048]{1,0:T(8,128)(2,1)}, bf16[512,2048]{1,0:T(8,128)(2,1)}, u32[]{:S(2)}, u32[]{:S(2)}) collective-permute-start(bf16[512,2048]{1,0:T(8,128)(2,1)} %get-tuple-element.30), channel_id=1, source_target_pairs={{0,8},{8,0},{16,24},{24,16},{32,40},{40,32},{48,56},{56,48},{64,72... | collective-permute-start | bytes 6291464 | tf_op jit(solution)/shard_map/ppermute | solution.py:176
  79.5 7.5 %collective-permute-start.3 = (bf16[512,2048]{1,0:T(8,128)(2,1)}, bf16[512,2048]{1,0:T(8,128)(2,1)}, u32[]{:S(2)}, u32[]{:S(2)}) collective-permute-start(bf16[512,2048]{1,0:T(8,128)(2,1)} %get-tuple-element.29), channel_id=1, source_target_pairs={{0,8},{8,0},{16,24},{24,16},{32,40},{40,32},{48,56},{56,48},{64,72... | collective-permute-start | bytes 6291464 | tf_op jit(solution)/shard_map/ppermute | solution.py:177
  83.5 3.5 %copy-start.13 = (bf16[1,256,2048]{2,1,0:T(8,128)(2,1)S(1)}, bf16[1,256,2048]{2,1,0:T(8,128)(2,1)}, u32[]{:S(2)}) copy-start(bf16[1,256,2048]{2,1,0:T(8,128)(2,1)} %param.17) | copy-start | bytes 3145732
  86.4 3.2 %copy-start.18 = (f32[2048]{0:T(1024)S(1)}, f32[2048]{0:T(1024)}, u32[]{:S(2)}) copy-start(f32[2048]{0:T(1024)} %param.19) | copy-start | bytes 24580
  89.6 1.3 copy-start.2
  90.9 46.7 %copy-start.9 = (bf16[1,2048,384]{2,1,0:T(8,128)(2,1)S(1)}, bf16[1,2048,384]{2,1,0:T(8,128)(2,1)}, u32[]{:S(2)}) copy-start(bf16[1,2048,384]{2,1,0:T(8,128)(2,1)} %param.22) | copy-start | bytes 4718596
  137.6 1.8 copy-start.10
  141.4 3.5 %copy-start.22 = (bf16[32,1,24,384]{3,2,0,1:T(8,128)(2,1)}, bf16[32,1,24,384]{3,2,0,1:T(8,128)(2,1)S(1)}, u32[]{:S(2)}) copy-start(bf16[32,1,24,384]{3,2,0,1:T(8,128)(2,1)S(1)} %get-tuple-element.26) | copy-start | bytes 1769476
  148.9 1.9 copy-start.16
  148.9 1.9 copy-start.14
  154.7 46.1 %all-to-all-start.2 = ((bf16[32,24,2048]{2,1,0:T(8,128)(2,1)}), bf16[32,24,2048]{2,1,0:T(8,128)(2,1)S(1)}, u32[]{:S(2)}, u32[]{:S(2)}) async-start(bf16[32,24,2048]{2,1,0:T(8,128)(2,1)} %bitcast.223), calls=%async_computation.2 | async-start | bytes 6291456 | tf_op jit(solution)/shard_map/all_to_all | solution.py:199
  159.0 3.6 %copy-start.11 = (bf16[1,2048,384]{2,1,0:T(8,128)(2,1)S(1)}, bf16[1,2048,384]{2,1,0:T(8,128)(2,1)}, u32[]{:S(2)}) copy-start(bf16[1,2048,384]{2,1,0:T(8,128)(2,1)} %param.23) | copy-start | bytes 4718596
  159.0 3.6 %copy-start.15 = (bf16[32,1,24,384]{3,2,0,1:T(8,128)(2,1)S(1)}, bf16[32,1,24,384]{3,2,0,1:T(8,128)(2,1)}, u32[]{:S(2)}) copy-start(bf16[32,1,24,384]{3,2,0,1:T(8,128)(2,1)} %copy-done.14) | copy-start | bytes 1769476
  200.8 9.6 %copy-start.5 = (bf16[32,24,2048]{2,1,0:T(8,128)(2,1)}, bf16[32,24,2048]{2,1,0:T(8,128)(2,1)S(1)}, u32[]{:S(2)}) copy-start(bf16[32,24,2048]{2,1,0:T(8,128)(2,1)S(1)} %all-to-all-done.2) | copy-start | bytes 9437188
  200.8 46.8 %all-to-all-start.3 = ((bf16[32,24,2048]{2,1,0:T(8,128)(2,1)}), bf16[32,24,2048]{2,1,0:T(8,128)(2,1)}, u32[]{:S(2)}, u32[]{:S(2)}) async-start(bf16[32,24,2048]{2,1,0:T(8,128)(2,1)} %bitcast.221), calls=%async_computation.3 | async-start | bytes 6291456 | tf_op jit(solution)/shard_map/all_to_all | solution.py:206
  205.7 48.6 %reduce-scatter.5.cloned.1.call-start = ((), (), s32[]{:S(2)}) async-start(), calls=%async_computation.8 | async-start | bytes 1769472 | tf_op jit(solution)/shard_map/reduce_scatter | solution.py:237
  210.4 3.1 %copy-start.3 = (f32[256,2048]{1,0:T(8,128)S(1)}, f32[256,2048]{1,0:T(8,128)}, u32[]{:S(2)}) copy-start(f32[256,2048]{1,0:T(8,128)} %copy-done.2) | copy-start | bytes 6291460
  210.4 3.5 %copy-start.6 = (bf16[32,24,2048]{2,1,0:T(8,128)(2,1)S(1)}, bf16[32,24,2048]{2,1,0:T(8,128)(2,1)}, u32[]{:S(2)}) copy-start(bf16[32,24,2048]{2,1,0:T(8,128)(2,1)} %copy-done.5) | copy-start | bytes 9437188
  247.7 3.2 %copy-start.4 = (f32[256,2048]{1,0:T(8,128)S(1)}, f32[256,2048]{1,0:T(8,128)}, u32[]{:S(2)}) copy-start(f32[256,2048]{1,0:T(8,128)} %copy-done.2) | copy-start | bytes 6291460
  247.7 3.2 %copy-start.8 = (bf16[1,256,2048]{2,1,0:T(8,128)(2,1)S(1)}, bf16[1,256,2048]{2,1,0:T(8,128)(2,1)}, u32[]{:S(2)}) copy-start(bf16[1,256,2048]{2,1,0:T(8,128)(2,1)} %param.25) | copy-start | bytes 3145732
  250.9 3.4 %copy-start.1 = (bf16[1,384,2048]{2,1,0:T(8,128)(2,1)S(1)}, bf16[1,384,2048]{2,1,0:T(8,128)(2,1)}, u32[]{:S(2)}) copy-start(bf16[1,384,2048]{2,1,0:T(8,128)(2,1)} %param.24) | copy-start | bytes 4718596
Sparse Core Ops, SparseCore 0:
  10.3 64.4 all-gather.1
  154.9 41.7 reduce-scatter.2
  210.5 39.0 reduce-scatter.4
